TPU v7x, 256 devices: a whole 4x4x8 slice. The times are simulated.
256 devices in a mesh: seq: 32 (over z_lo, y, core), head: 8 (over x, z_hi).
Axes of the slice: x: 4, y: 4, z: 8 (z_hi: 2, z_lo: 4; z = z_hi * 4 + z_lo), core: 2. Of those that a mesh axis runs over, the one named last changes fastest.
Arguments:
- queries: bfloat16 [16384, 1024], P('seq', 'head'), may hold values from -2.5 to 2.5
- keys: bfloat16 [16384, 1024], P('seq', 'head'), may hold values from -2.5 to 2.5
- values: bfloat16 [16384, 1024], P('seq', 'head'), may hold values from -6 to 6
- attn_out: bfloat16 [16384, 1024], P('seq', 'head'), may hold values from -6 to 6
- out_grad: bfloat16 [16384, 1024], P('seq', 'head'), may hold values from -6 to 6
- lse: float32 [8, 16384], P('head', 'seq'), may hold values from 3.5 to 5.5
- trace_id: int32 [16384], replicated, may hold values from 0 to 127, never falling along the last dimension, each value on 1 to 384 neighbouring positions
- key_tiles: int32 [128, 48], P('seq'), may hold values from 0 to 127, as said below
- tile_count: int32 [128], P('seq'), may hold values from 1 to 48, as said below
- w_query: bfloat16 [1024, 1024], P(None, 'head'), may hold values from -0.1875 to 0.1875
- w_key: bfloat16 [1024, 1024], P(None, 'head'), may hold values from -0.1875 to 0.1875
- w_value: bfloat16 [1024, 1024], P(None, 'head'), may hold values from -0.1875 to 0.1875
- w_out: bfloat16 [1024, 1024], P('head'), may hold values from -0.1875 to 0.1875
Outputs:
- d_input: bfloat16 [16384, 1024], P('seq', 'head')
Inputs may be any that keep to these rules, and one draw needn't show every extreme that they name: `key_tiles`: each row lists 48 different key tiles and never its own tile; entries from position tile_count onward are not used. `tile_count`: some query tile uses all 48 entries. `trace_id`: trace numbers never fall along the tokens; one trace spans 384 tokens, none more.
All inputs are finite; a program needn't handle non-finite values.
Results may differ from a plain program's by a relative error of at most 0.015.
Values may be sent and summed in bfloat16 or wider, within the bound.
No kernel may reach another device: no remote copies, remote signals or barrier semaphores. Data moves between devices by JAX's collectives and lax.ppermute only.
A program may use at most 64 MiB of HBM per device.

v0:
```python
import jax
import jax.numpy as jnp
from jax import lax
from jax.sharding import PartitionSpec as P

HD = 128
TILE = 128
SEL = 48


def from_behind(value, axis, by):
    count = lax.axis_size(axis)
    return lax.ppermute(value, axis, [(i, (i + by) % count) for i in range(count)])


def pair_grads(query_heads, key_heads, value_heads, grad_heads, norm_rows, delta_rows, admit):
    scale = query_heads.shape[-1] ** (-0.5)
    scores = (
        jnp.einsum("rhd,chd->hrc", query_heads, key_heads, preferred_element_type=jnp.float32)
        * scale
    )
    probs = jnp.where(admit[None], jnp.exp(scores - norm_rows[:, :, None]), 0.0)
    value_grad = jnp.einsum(
        "hrc,rhd->chd", probs.astype(jnp.bfloat16), grad_heads, preferred_element_type=jnp.float32
    )
    prob_grad = jnp.einsum(
        "rhd,chd->hrc", grad_heads, value_heads, preferred_element_type=jnp.float32
    )
    score_grad = (probs * (prob_grad - delta_rows[:, :, None]) * scale).astype(jnp.bfloat16)
    query_grad = jnp.einsum(
        "hrc,chd->rhd", score_grad, key_heads, preferred_element_type=jnp.float32
    )
    key_grad = jnp.einsum(
        "hrc,rhd->chd", score_grad, query_heads, preferred_element_type=jnp.float32
    )
    return (query_grad, key_grad, value_grad)


def settle(total):
    part = lax.optimization_barrier(total.astype(jnp.bfloat16))
    return part.astype(jnp.float32)


def per_device(
    queries,
    keys,
    values,
    attn_out,
    out_grad,
    lse,
    trace_id,
    key_tiles,
    tile_count,
    w_query,
    w_key,
    w_value,
    w_out,
):
    tokens_here, width = queries.shape
    heads_here = width // HD
    seq_count = lax.axis_size("seq")
    seq_index = lax.axis_index("seq")
    tiles_here = tokens_here // TILE
    d_attn = lax.dot_general(
        lax.all_gather(out_grad, "head", axis=1, tiled=True),
        w_out,
        (((1,), (1,)), ((), ())),
        preferred_element_type=jnp.float32,
    ).astype(jnp.bfloat16)
    product = d_attn.astype(jnp.float32) * attn_out.astype(jnp.float32)
    delta = jnp.sum(product.reshape(tokens_here, heads_here, HD), axis=2).T
    query_heads = queries.reshape(tokens_here, heads_here, HD)
    key_heads = keys.reshape(tokens_here, heads_here, HD)
    value_heads = values.reshape(tokens_here, heads_here, HD)
    grad_heads = d_attn.reshape(tokens_here, heads_here, HD)
    trace_here = lax.dynamic_slice_in_dim(trace_id, seq_index * tokens_here, tokens_here, 0)
    slots = jnp.arange(SEL)[None, :] < tile_count[:, None]
    tile_range = jnp.arange(seq_count * tiles_here)
    allowed = jnp.any(
        (key_tiles[:, :, None] == tile_range[None, None, :]) & slots[:, :, None], axis=1
    )

    def visit(key_block, value_block, first_tile):
        block_tiles = key_block.shape[0] // TILE
        listed = lax.dynamic_slice(allowed, (0, first_tile), (tiles_here, block_tiles))
        trace_keys = lax.dynamic_slice_in_dim(trace_id, first_tile * TILE, key_block.shape[0], 0)
        admit = jnp.repeat(jnp.repeat(listed, TILE, axis=0), TILE, axis=1) & (
            trace_here[:, None] != trace_keys[None, :]
        )
        return pair_grads(query_heads, key_block, value_block, grad_heads, lse, delta, admit)

    zero_rows = jnp.zeros((tokens_here, heads_here, HD), jnp.float32)

    def pass_sums(sums):
        return from_behind(sums, "seq", 1)

    def cycle_work(step, held, sums, query_sum):
        source = (seq_index - step) % seq_count
        query_add, key_add, value_add = visit(held[0], held[1], source * tiles_here)
        return (query_sum + query_add, sums + jnp.stack([settle(key_add), settle(value_add)]))

    def cycle_turn(step, carry):
        held, sums, query_sum = carry
        query_sum, sums = cycle_work(step, held, sums, query_sum)
        held = from_behind(held, "seq", 1)
        return (held, pass_sums(sums), query_sum)

    start_carry = (
        jnp.stack([key_heads, value_heads]),
        jnp.stack([zero_rows, zero_rows]),
        zero_rows,
    )
    held, sums, query_sum = lax.fori_loop(0, seq_count - 1, cycle_turn, start_carry)
    query_sum, sums = cycle_work(seq_count - 1, held, sums, query_sum)
    sums = pass_sums(sums)
    key_sum, value_sum = (sums[0], sums[1])
    d_query = query_sum.astype(jnp.bfloat16).reshape(tokens_here, width)
    d_key = key_sum.astype(jnp.bfloat16).reshape(tokens_here, width)
    d_value = value_sum.astype(jnp.bfloat16).reshape(tokens_here, width)
    contract = (((1,), (1,)), ((), ()))
    total = lax.dot_general(w_query, d_query, contract, preferred_element_type=jnp.float32)
    total = total + lax.dot_general(w_key, d_key, contract, preferred_element_type=jnp.float32)
    d_input = lax.psum_scatter(
        total + lax.dot_general(w_value, d_value, contract, preferred_element_type=jnp.float32),
        "head",
        scatter_dimension=0,
        tiled=True,
    )
    return d_input.T.astype(jnp.bfloat16)


def solution(mesh):
    in_specs = (
        P("seq", "head"),
        P("seq", "head"),
        P("seq", "head"),
        P("seq", "head"),
        P("seq", "head"),
        P("head", "seq"),
        P(),
        P("seq", None),
        P("seq"),
        P(None, "head"),
        P(None, "head"),
        P(None, "head"),
        P("head", None),
    )
    out_specs = P("seq", "head")
    return jax.shard_map(
        per_device, mesh=mesh, in_specs=in_specs, out_specs=out_specs, check_vma=False
    )
```

profile of v0, /device:TPU:8, one launch (start us, length us, event | category | flops | bytes accessed | tf_op | source)
XLA Modules:
  0.0 790.5 jit_solution(7173864981957476666)
XLA Ops:
  12.3 61.9 %all-gather.2.cloned.1.call-done = bf16[512,1024]{1,0:T(8,128)(2,1)} async-done(((bf16[512,128]{1,0:T(8,128)(2,1)}), bf16[512,1024]{1,0:T(8,128)(2,1)}) %all-gather.2.cloned.1.call-update) | async-done | bytes 1048592 | tf_op jit(solution)/shard_map/all_gather | solution.py:65
  74.2 1.8 multiply_reduce_fusion
  76.2 585.5 %while.20 = (s32[]{:T(128)}, bf16[2,512,1,128]{3,1,2,0:T(8,128)(2,1)S(1)}, f32[2,512,1,128]{3,1,2,0:T(8,128)S(1)}, f32[512,1,128]{2,0,1:T(8,128)S(1)}, s32[]{:T(...) while((s32[]{:T(128)}, ...), condition=%wide.region_3.4_spmd.clone, body=%wide.region_2.3_spmd.clone.sunk | while | flops 338821152 | bytes 11944476 | solution.py:113
  77.1 1.6 broadcast_in_dim.75
  82.3 9.5 %collective-permute-done = bf16[2,512,1,128]{3,1,2,0:T(8,128)(2,1)S(1)} collective-permute-done((bf16[2,512,1,128]{3,1,2,0:T(8,128)(2,1)S(1)}, bf16[2,512,1,128]{3,1,2,0:T(8,128)(2,1)S(1)}, u32[]{:S(2)}, u32[]{:S(2)}) %collective-permute-start) | collective-permute-done | bytes 262176 | tf_op jit(solution)/shard_map/while/body/eval_jaxpr/ppermute | solution.py:13
  92.7 1.6 broadcast_in_dim.75
  97.9 9.5 %collective-permute-done = bf16[2,512,1,128]{3,1,2,0:T(8,128)(2,1)S(1)} collective-permute-done((bf16[2,512,1,128]{3,1,2,0:T(8,128)(2,1)S(1)}, bf16[2,512,1,128]{3,1,2,0:T(8,128)(2,1)S(1)}, u32[]{:S(2)}, u32[]{:S(2)}) %collective-permute-start) | collective-permute-done | bytes 262176 | tf_op jit(solution)/shard_map/while/body/eval_jaxpr/ppermute | solution.py:13
  108.3 1.6 broadcast_in_dim.75
  113.5 9.5 %collective-permute-done = bf16[2,512,1,128]{3,1,2,0:T(8,128)(2,1)S(1)} collective-permute-done((bf16[2,512,1,128]{3,1,2,0:T(8,128)(2,1)S(1)}, bf16[2,512,1,128]{3,1,2,0:T(8,128)(2,1)S(1)}, u32[]{:S(2)}, u32[]{:S(2)}) %collective-permute-start) | collective-permute-done | bytes 262176 | tf_op jit(solution)/shard_map/while/body/eval_jaxpr/ppermute | solution.py:13
  123.8 1.6 broadcast_in_dim.75
  129.0 9.5 %collective-permute-done = bf16[2,512,1,128]{3,1,2,0:T(8,128)(2,1)S(1)} collective-permute-done((bf16[2,512,1,128]{3,1,2,0:T(8,128)(2,1)S(1)}, bf16[2,512,1,128]{3,1,2,0:T(8,128)(2,1)S(1)}, u32[]{:S(2)}, u32[]{:S(2)}) %collective-permute-start) | collective-permute-done | bytes 262176 | tf_op jit(solution)/shard_map/while/body/eval_jaxpr/ppermute | solution.py:13
  139.4 1.6 broadcast_in_dim.75
  144.6 10.5 %collective-permute-done = bf16[2,512,1,128]{3,1,2,0:T(8,128)(2,1)S(1)} collective-permute-done((bf16[2,512,1,128]{3,1,2,0:T(8,128)(2,1)S(1)}, bf16[2,512,1,128]{3,1,2,0:T(8,128)(2,1)S(1)}, u32[]{:S(2)}, u32[]{:S(2)}) %collective-permute-start) | collective-permute-done | bytes 262176 | tf_op jit(solution)/shard_map/while/body/eval_jaxpr/ppermute | solution.py:13
  156.0 1.6 broadcast_in_dim.75
  160.2 14.4 %collective-permute-done = bf16[2,512,1,128]{3,1,2,0:T(8,128)(2,1)S(1)} collective-permute-done((bf16[2,512,1,128]{3,1,2,0:T(8,128)(2,1)S(1)}, bf16[2,512,1,128]{3,1,2,0:T(8,128)(2,1)S(1)}, u32[]{:S(2)}, u32[]{:S(2)}) %collective-permute-start) | collective-permute-done | bytes 262176 | tf_op jit(solution)/shard_map/while/body/eval_jaxpr/ppermute | solution.py:13
  175.5 1.6 broadcast_in_dim.75
  179.2 14.9 %collective-permute-done = bf16[2,512,1,128]{3,1,2,0:T(8,128)(2,1)S(1)} collective-permute-done((bf16[2,512,1,128]{3,1,2,0:T(8,128)(2,1)S(1)}, bf16[2,512,1,128]{3,1,2,0:T(8,128)(2,1)S(1)}, u32[]{:S(2)}, u32[]{:S(2)}) %collective-permute-start) | collective-permute-done | bytes 262176 | tf_op jit(solution)/shard_map/while/body/eval_jaxpr/ppermute | solution.py:13
  195.0 1.6 broadcast_in_dim.75
  198.7 14.9 %collective-permute-done = bf16[2,512,1,128]{3,1,2,0:T(8,128)(2,1)S(1)} collective-permute-done((bf16[2,512,1,128]{3,1,2,0:T(8,128)(2,1)S(1)}, bf16[2,512,1,128]{3,1,2,0:T(8,128)(2,1)S(1)}, u32[]{:S(2)}, u32[]{:S(2)}) %collective-permute-start) | collective-permute-done | bytes 262176 | tf_op jit(solution)/shard_map/while/body/eval_jaxpr/ppermute | solution.py:13
  214.4 1.6 broadcast_in_dim.75
  218.1 14.9 %collective-permute-done = bf16[2,512,1,128]{3,1,2,0:T(8,128)(2,1)S(1)} collective-permute-done((bf16[2,512,1,128]{3,1,2,0:T(8,128)(2,1)S(1)}, bf16[2,512,1,128]{3,1,2,0:T(8,128)(2,1)S(1)}, u32[]{:S(2)}, u32[]{:S(2)}) %collective-permute-start) | collective-permute-done | bytes 262176 | tf_op jit(solution)/shard_map/while/body/eval_jaxpr/ppermute | solution.py:13
  237.6 14.9 %collective-permute-done = bf16[2,512,1,128]{3,1,2,0:T(8,128)(2,1)S(1)} collective-permute-done((bf16[2,512,1,128]{3,1,2,0:T(8,128)(2,1)S(1)}, bf16[2,512,1,128]{3,1,2,0:T(8,128)(2,1)S(1)}, u32[]{:S(2)}, u32[]{:S(2)}) %collective-permute-start) | collective-permute-done | bytes 262176 | tf_op jit(solution)/shard_map/while/body/eval_jaxpr/ppermute | solution.py:13
  253.4 1.6 broadcast_in_dim.75
  257.1 14.9 %collective-permute-done = bf16[2,512,1,128]{3,1,2,0:T(8,128)(2,1)S(1)} collective-permute-done((bf16[2,512,1,128]{3,1,2,0:T(8,128)(2,1)S(1)}, bf16[2,512,1,128]{3,1,2,0:T(8,128)(2,1)S(1)}, u32[]{:S(2)}, u32[]{:S(2)}) %collective-permute-start) | collective-permute-done | bytes 262176 | tf_op jit(solution)/shard_map/while/body/eval_jaxpr/ppermute | solution.py:13
  272.9 1.6 broadcast_in_dim.75
  276.6 14.9 %collective-permute-done = bf16[2,512,1,128]{3,1,2,0:T(8,128)(2,1)S(1)} collective-permute-done((bf16[2,512,1,128]{3,1,2,0:T(8,128)(2,1)S(1)}, bf16[2,512,1,128]{3,1,2,0:T(8,128)(2,1)S(1)}, u32[]{:S(2)}, u32[]{:S(2)}) %collective-permute-start) | collective-permute-done | bytes 262176 | tf_op jit(solution)/shard_map/while/body/eval_jaxpr/ppermute | solution.py:13
  292.4 1.6 broadcast_in_dim.75
  296.1 14.9 %collective-permute-done = bf16[2,512,1,128]{3,1,2,0:T(8,128)(2,1)S(1)} collective-permute-done((bf16[2,512,1,128]{3,1,2,0:T(8,128)(2,1)S(1)}, bf16[2,512,1,128]{3,1,2,0:T(8,128)(2,1)S(1)}, u32[]{:S(2)}, u32[]{:S(2)}) %collective-permute-start) | collective-permute-done | bytes 262176 | tf_op jit(solution)/shard_map/while/body/eval_jaxpr/ppermute | solution.py:13
  315.5 14.9 %collective-permute-done = bf16[2,512,1,128]{3,1,2,0:T(8,128)(2,1)S(1)} collective-permute-done((bf16[2,512,1,128]{3,1,2,0:T(8,128)(2,1)S(1)}, bf16[2,512,1,128]{3,1,2,0:T(8,128)(2,1)S(1)}, u32[]{:S(2)}, u32[]{:S(2)}) %collective-permute-start) | collective-permute-done | bytes 262176 | tf_op jit(solution)/shard_map/while/body/eval_jaxpr/ppermute | solution.py:13
  331.3 1.6 broadcast_in_dim.75
  335.0 14.9 %collective-permute-done = bf16[2,512,1,128]{3,1,2,0:T(8,128)(2,1)S(1)} collective-permute-done((bf16[2,512,1,128]{3,1,2,0:T(8,128)(2,1)S(1)}, bf16[2,512,1,128]{3,1,2,0:T(8,128)(2,1)S(1)}, u32[]{:S(2)}, u32[]{:S(2)}) %collective-permute-start) | collective-permute-done | bytes 262176 | tf_op jit(solution)/shard_map/while/body/eval_jaxpr/ppermute | solution.py:13
  350.8 1.6 broadcast_in_dim.75
  354.5 14.9 %collective-permute-done = bf16[2,512,1,128]{3,1,2,0:T(8,128)(2,1)S(1)} collective-permute-done((bf16[2,512,1,128]{3,1,2,0:T(8,128)(2,1)S(1)}, bf16[2,512,1,128]{3,1,2,0:T(8,128)(2,1)S(1)}, u32[]{:S(2)}, u32[]{:S(2)}) %collective-permute-start) | collective-permute-done | bytes 262176 | tf_op jit(solution)/shard_map/while/body/eval_jaxpr/ppermute | solution.py:13
  370.3 1.6 broadcast_in_dim.75
  374.0 14.9 %collective-permute-done = bf16[2,512,1,128]{3,1,2,0:T(8,128)(2,1)S(1)} collective-permute-done((bf16[2,512,1,128]{3,1,2,0:T(8,128)(2,1)S(1)}, bf16[2,512,1,128]{3,1,2,0:T(8,128)(2,1)S(1)}, u32[]{:S(2)}, u32[]{:S(2)}) %collective-permute-start) | collective-permute-done | bytes 262176 | tf_op jit(solution)/shard_map/while/body/eval_jaxpr/ppermute | solution.py:13
  393.5 14.9 %collective-permute-done = bf16[2,512,1,128]{3,1,2,0:T(8,128)(2,1)S(1)} collective-permute-done((bf16[2,512,1,128]{3,1,2,0:T(8,128)(2,1)S(1)}, bf16[2,512,1,128]{3,1,2,0:T(8,128)(2,1)S(1)}, u32[]{:S(2)}, u32[]{:S(2)}) %collective-permute-start) | collective-permute-done | bytes 262176 | tf_op jit(solution)/shard_map/while/body/eval_jaxpr/ppermute | solution.py:13
  409.3 1.6 broadcast_in_dim.75
  413.0 14.9 %collective-permute-done = bf16[2,512,1,128]{3,1,2,0:T(8,128)(2,1)S(1)} collective-permute-done((bf16[2,512,1,128]{3,1,2,0:T(8,128)(2,1)S(1)}, bf16[2,512,1,128]{3,1,2,0:T(8,128)(2,1)S(1)}, u32[]{:S(2)}, u32[]{:S(2)}) %collective-permute-start) | collective-permute-done | bytes 262176 | tf_op jit(solution)/shard_map/while/body/eval_jaxpr/ppermute | solution.py:13
  428.7 1.6 broadcast_in_dim.75
  432.4 14.9 %collective-permute-done = bf16[2,512,1,128]{3,1,2,0:T(8,128)(2,1)S(1)} collective-permute-done((bf16[2,512,1,128]{3,1,2,0:T(8,128)(2,1)S(1)}, bf16[2,512,1,128]{3,1,2,0:T(8,128)(2,1)S(1)}, u32[]{:S(2)}, u32[]{:S(2)}) %collective-permute-start) | collective-permute-done | bytes 262176 | tf_op jit(solution)/shard_map/while/body/eval_jaxpr/ppermute | solution.py:13
  448.2 1.6 broadcast_in_dim.75
  451.9 14.9 %collective-permute-done = bf16[2,512,1,128]{3,1,2,0:T(8,128)(2,1)S(1)} collective-permute-done((bf16[2,512,1,128]{3,1,2,0:T(8,128)(2,1)S(1)}, bf16[2,512,1,128]{3,1,2,0:T(8,128)(2,1)S(1)}, u32[]{:S(2)}, u32[]{:S(2)}) %collective-permute-start) | collective-permute-done | bytes 262176 | tf_op jit(solution)/shard_map/while/body/eval_jaxpr/ppermute | solution.py:13
  471.4 14.9 %collective-permute-done = bf16[2,512,1,128]{3,1,2,0:T(8,128)(2,1)S(1)} collective-permute-done((bf16[2,512,1,128]{3,1,2,0:T(8,128)(2,1)S(1)}, bf16[2,512,1,128]{3,1,2,0:T(8,128)(2,1)S(1)}, u32[]{:S(2)}, u32[]{:S(2)}) %collective-permute-start) | collective-permute-done | bytes 262176 | tf_op jit(solution)/shard_map/while/body/eval_jaxpr/ppermute | solution.py:13
  487.2 1.6 broadcast_in_dim.75
  490.9 14.9 %collective-permute-done = bf16[2,512,1,128]{3,1,2,0:T(8,128)(2,1)S(1)} collective-permute-done((bf16[2,512,1,128]{3,1,2,0:T(8,128)(2,1)S(1)}, bf16[2,512,1,128]{3,1,2,0:T(8,128)(2,1)S(1)}, u32[]{:S(2)}, u32[]{:S(2)}) %collective-permute-start) | collective-permute-done | bytes 262176 | tf_op jit(solution)/shard_map/while/body/eval_jaxpr/ppermute | solution.py:13
  506.7 1.6 broadcast_in_dim.75
  510.4 14.9 %collective-permute-done = bf16[2,512,1,128]{3,1,2,0:T(8,128)(2,1)S(1)} collective-permute-done((bf16[2,512,1,128]{3,1,2,0:T(8,128)(2,1)S(1)}, bf16[2,512,1,128]{3,1,2,0:T(8,128)(2,1)S(1)}, u32[]{:S(2)}, u32[]{:S(2)}) %collective-permute-start) | collective-permute-done | bytes 262176 | tf_op jit(solution)/shard_map/while/body/eval_jaxpr/ppermute | solution.py:13
  526.1 1.6 broadcast_in_dim.75
  529.9 14.9 %collective-permute-done = bf16[2,512,1,128]{3,1,2,0:T(8,128)(2,1)S(1)} collective-permute-done((bf16[2,512,1,128]{3,1,2,0:T(8,128)(2,1)S(1)}, bf16[2,512,1,128]{3,1,2,0:T(8,128)(2,1)S(1)}, u32[]{:S(2)}, u32[]{:S(2)}) %collective-permute-start) | collective-permute-done | bytes 262176 | tf_op jit(solution)/shard_map/while/body/eval_jaxpr/ppermute | solution.py:13
  549.3 14.9 %collective-permute-done = bf16[2,512,1,128]{3,1,2,0:T(8,128)(2,1)S(1)} collective-permute-done((bf16[2,512,1,128]{3,1,2,0:T(8,128)(2,1)S(1)}, bf16[2,512,1,128]{3,1,2,0:T(8,128)(2,1)S(1)}, u32[]{:S(2)}, u32[]{:S(2)}) %collective-permute-start) | collective-permute-done | bytes 262176 | tf_op jit(solution)/shard_map/while/body/eval_jaxpr/ppermute | solution.py:13
  565.1 1.6 broadcast_in_dim.75
  568.8 14.9 %collective-permute-done = bf16[2,512,1,128]{3,1,2,0:T(8,128)(2,1)S(1)} collective-permute-done((bf16[2,512,1,128]{3,1,2,0:T(8,128)(2,1)S(1)}, bf16[2,512,1,128]{3,1,2,0:T(8,128)(2,1)S(1)}, u32[]{:S(2)}, u32[]{:S(2)}) %collective-permute-start) | collective-permute-done | bytes 262176 | tf_op jit(solution)/shard_map/while/body/eval_jaxpr/ppermute | solution.py:13
  584.6 1.6 broadcast_in_dim.75
  588.3 14.9 %collective-permute-done = bf16[2,512,1,128]{3,1,2,0:T(8,128)(2,1)S(1)} collective-permute-done((bf16[2,512,1,128]{3,1,2,0:T(8,128)(2,1)S(1)}, bf16[2,512,1,128]{3,1,2,0:T(8,128)(2,1)S(1)}, u32[]{:S(2)}, u32[]{:S(2)}) %collective-permute-start) | collective-permute-done | bytes 262176 | tf_op jit(solution)/shard_map/while/body/eval_jaxpr/ppermute | solution.py:13
  607.8 14.9 %collective-permute-done = bf16[2,512,1,128]{3,1,2,0:T(8,128)(2,1)S(1)} collective-permute-done((bf16[2,512,1,128]{3,1,2,0:T(8,128)(2,1)S(1)}, bf16[2,512,1,128]{3,1,2,0:T(8,128)(2,1)S(1)}, u32[]{:S(2)}, u32[]{:S(2)}) %collective-permute-start) | collective-permute-done | bytes 262176 | tf_op jit(solution)/shard_map/while/body/eval_jaxpr/ppermute | solution.py:13
  623.6 1.6 broadcast_in_dim.75
  627.3 14.9 %collective-permute-done = bf16[2,512,1,128]{3,1,2,0:T(8,128)(2,1)S(1)} collective-permute-done((bf16[2,512,1,128]{3,1,2,0:T(8,128)(2,1)S(1)}, bf16[2,512,1,128]{3,1,2,0:T(8,128)(2,1)S(1)}, u32[]{:S(2)}, u32[]{:S(2)}) %collective-permute-start) | collective-permute-done | bytes 262176 | tf_op jit(solution)/shard_map/while/body/eval_jaxpr/ppermute | solution.py:13
  643.0 1.6 broadcast_in_dim.75
  646.7 14.9 %collective-permute-done = bf16[2,512,1,128]{3,1,2,0:T(8,128)(2,1)S(1)} collective-permute-done((bf16[2,512,1,128]{3,1,2,0:T(8,128)(2,1)S(1)}, bf16[2,512,1,128]{3,1,2,0:T(8,128)(2,1)S(1)}, u32[]{:S(2)}, u32[]{:S(2)}) %collective-permute-start) | collective-permute-done | bytes 262176 | tf_op jit(solution)/shard_map/while/body/eval_jaxpr/ppermute | solution.py:13
  663.3 2.0 fusion.32
  665.3 7.6 collective-permute-done.2
  673.4 1.8 add_bitcast_fusion
  675.2 106.9 %reduce-scatter.2.cloned.1.call-done = f32[128,512]{0,1:T(8,128)} async-done(((f32[1024,512]{0,1:T(8,128)}), f32[128,512]{0,1:T(8,128)}) %reduce-scatter.2.cloned.1.call-update) | async-done | bytes 262160 | tf_op jit(solution)/shard_map/reduce_scatter | solution.py:123
  782.0 1.6 convert_bitcast_fusion
  (446 shorter events, 115.9 us)
Async XLA Ops:
  6.5 67.7 %all-gather.2.cloned.1.call-start = ((), (), s32[]{:S(2)}) async-start(), calls=%async_computation.1 | async-start | bytes 1179648 | tf_op jit(solution)/shard_map/all_gather | solution.py:65
  7.3 774.8 %reduce-scatter.2.cloned.1.call-start = ((), (), s32[]{:S(2)}) async-start(), calls=%async_computation.2 | async-start | bytes 2359296 | tf_op jit(solution)/shard_map/reduce_scatter | solution.py:123
  80.3 11.5 %collective-permute-start.1 = (f32[2,512,1,128]{3,1,2,0:T(8,128)S(1)}, f32[2,512,1,128]{3,1,2,0:T(8,128)S(1)}, u32[]{:S(2)}, u32[]{:S(2)}) collective-permute-start(f32[2,512,1,128]{3,1,2,0:T(8,128)S(1)} %convert_add_fusion.3), channel_id=1, source_target_pairs={{0,8},{8,16},{16,24},{24,32},{32,40},{40,48},{48,56},{56,64},{64,7... | collective-permute-start | bytes 1572872 | tf_op jit(solution)/shard_map/while/body/eval_jaxpr/ppermute | solution.py:13
  80.4 11.4 %collective-permute-start = (bf16[2,512,1,128]{3,1,2,0:T(8,128)(2,1)S(1)}, bf16[2,512,1,128]{3,1,2,0:T(8,128)(2,1)S(1)}, u32[]{:S(2)}, u32[]{:S(2)}) collective-permute-start(bf16[2,512,1,128]{3,1,2,0:T(8,128)(2,1)S(1)} %copy.49), channel_id=1, source_target_pairs={{0,8},{8,16},{16,24},{24,32},{32,40},{40,48},{48,56},{56,64},{64,7... | collective-permute-start | bytes 786440 | tf_op jit(solution)/shard_map/while/body/eval_jaxpr/ppermute | solution.py:13
  95.9 11.5 %collective-permute-start.1 = (f32[2,512,1,128]{3,1,2,0:T(8,128)S(1)}, f32[2,512,1,128]{3,1,2,0:T(8,128)S(1)}, u32[]{:S(2)}, u32[]{:S(2)}) collective-permute-start(f32[2,512,1,128]{3,1,2,0:T(8,128)S(1)} %convert_add_fusion.3), channel_id=1, source_target_pairs={{0,8},{8,16},{16,24},{24,32},{32,40},{40,48},{48,56},{56,64},{64,7... | collective-permute-start | bytes 1572872 | tf_op jit(solution)/shard_map/while/body/eval_jaxpr/ppermute | solution.py:13
  96.0 11.4 %collective-permute-start = (bf16[2,512,1,128]{3,1,2,0:T(8,128)(2,1)S(1)}, bf16[2,512,1,128]{3,1,2,0:T(8,128)(2,1)S(1)}, u32[]{:S(2)}, u32[]{:S(2)}) collective-permute-start(bf16[2,512,1,128]{3,1,2,0:T(8,128)(2,1)S(1)} %copy.49), channel_id=1, source_target_pairs={{0,8},{8,16},{16,24},{24,32},{32,40},{40,48},{48,56},{56,64},{64,7... | collective-permute-start | bytes 786440 | tf_op jit(solution)/shard_map/while/body/eval_jaxpr/ppermute | solution.py:13
  111.4 11.5 %collective-permute-start.1 = (f32[2,512,1,128]{3,1,2,0:T(8,128)S(1)}, f32[2,512,1,128]{3,1,2,0:T(8,128)S(1)}, u32[]{:S(2)}, u32[]{:S(2)}) collective-permute-start(f32[2,512,1,128]{3,1,2,0:T(8,128)S(1)} %convert_add_fusion.3), channel_id=1, source_target_pairs={{0,8},{8,16},{16,24},{24,32},{32,40},{40,48},{48,56},{56,64},{64,7... | collective-permute-start | bytes 1572872 | tf_op jit(solution)/shard_map/while/body/eval_jaxpr/ppermute | solution.py:13
  111.5 11.4 %collective-permute-start = (bf16[2,512,1,128]{3,1,2,0:T(8,128)(2,1)S(1)}, bf16[2,512,1,128]{3,1,2,0:T(8,128)(2,1)S(1)}, u32[]{:S(2)}, u32[]{:S(2)}) collective-permute-start(bf16[2,512,1,128]{3,1,2,0:T(8,128)(2,1)S(1)} %copy.49), channel_id=1, source_target_pairs={{0,8},{8,16},{16,24},{24,32},{32,40},{40,48},{48,56},{56,64},{64,7... | collective-permute-start | bytes 786440 | tf_op jit(solution)/shard_map/while/body/eval_jaxpr/ppermute | solution.py:13
  127.0 11.5 %collective-permute-start.1 = (f32[2,512,1,128]{3,1,2,0:T(8,128)S(1)}, f32[2,512,1,128]{3,1,2,0:T(8,128)S(1)}, u32[]{:S(2)}, u32[]{:S(2)}) collective-permute-start(f32[2,512,1,128]{3,1,2,0:T(8,128)S(1)} %convert_add_fusion.3), channel_id=1, source_target_pairs={{0,8},{8,16},{16,24},{24,32},{32,40},{40,48},{48,56},{56,64},{64,7... | collective-permute-start | bytes 1572872 | tf_op jit(solution)/shard_map/while/body/eval_jaxpr/ppermute | solution.py:13
  127.1 11.4 %collective-permute-start = (bf16[2,512,1,128]{3,1,2,0:T(8,128)(2,1)S(1)}, bf16[2,512,1,128]{3,1,2,0:T(8,128)(2,1)S(1)}, u32[]{:S(2)}, u32[]{:S(2)}) collective-permute-start(bf16[2,512,1,128]{3,1,2,0:T(8,128)(2,1)S(1)} %copy.49), channel_id=1, source_target_pairs={{0,8},{8,16},{16,24},{24,32},{32,40},{40,48},{48,56},{56,64},{64,7... | collective-permute-start | bytes 786440 | tf_op jit(solution)/shard_map/while/body/eval_jaxpr/ppermute | solution.py:13
  142.6 12.5 %collective-permute-start.1 = (f32[2,512,1,128]{3,1,2,0:T(8,128)S(1)}, f32[2,512,1,128]{3,1,2,0:T(8,128)S(1)}, u32[]{:S(2)}, u32[]{:S(2)}) collective-permute-start(f32[2,512,1,128]{3,1,2,0:T(8,128)S(1)} %convert_add_fusion.3), channel_id=1, source_target_pairs={{0,8},{8,16},{16,24},{24,32},{32,40},{40,48},{48,56},{56,64},{64,7... | collective-permute-start | bytes 1572872 | tf_op jit(solution)/shard_map/while/body/eval_jaxpr/ppermute | solution.py:13
  142.7 12.4 %collective-permute-start = (bf16[2,512,1,128]{3,1,2,0:T(8,128)(2,1)S(1)}, bf16[2,512,1,128]{3,1,2,0:T(8,128)(2,1)S(1)}, u32[]{:S(2)}, u32[]{:S(2)}) collective-permute-start(bf16[2,512,1,128]{3,1,2,0:T(8,128)(2,1)S(1)} %copy.49), channel_id=1, source_target_pairs={{0,8},{8,16},{16,24},{24,32},{32,40},{40,48},{48,56},{56,64},{64,7... | collective-permute-start | bytes 786440 | tf_op jit(solution)/shard_map/while/body/eval_jaxpr/ppermute | solution.py:13
  159.2 15.4 %collective-permute-start.1 = (f32[2,512,1,128]{3,1,2,0:T(8,128)S(1)}, f32[2,512,1,128]{3,1,2,0:T(8,128)S(1)}, u32[]{:S(2)}, u32[]{:S(2)}) collective-permute-start(f32[2,512,1,128]{3,1,2,0:T(8,128)S(1)} %convert_add_fusion.3), channel_id=1, source_target_pairs={{0,8},{8,16},{16,24},{24,32},{32,40},{40,48},{48,56},{56,64},{64,7... | collective-permute-start | bytes 1572872 | tf_op jit(solution)/shard_map/while/body/eval_jaxpr/ppermute | solution.py:13
  159.3 15.3 %collective-permute-start = (bf16[2,512,1,128]{3,1,2,0:T(8,128)(2,1)S(1)}, bf16[2,512,1,128]{3,1,2,0:T(8,128)(2,1)S(1)}, u32[]{:S(2)}, u32[]{:S(2)}) collective-permute-start(bf16[2,512,1,128]{3,1,2,0:T(8,128)(2,1)S(1)} %copy.49), channel_id=1, source_target_pairs={{0,8},{8,16},{16,24},{24,32},{32,40},{40,48},{48,56},{56,64},{64,7... | collective-permute-start | bytes 786440 | tf_op jit(solution)/shard_map/while/body/eval_jaxpr/ppermute | solution.py:13
  178.7 15.4 %collective-permute-start.1 = (f32[2,512,1,128]{3,1,2,0:T(8,128)S(1)}, f32[2,512,1,128]{3,1,2,0:T(8,128)S(1)}, u32[]{:S(2)}, u32[]{:S(2)}) collective-permute-start(f32[2,512,1,128]{3,1,2,0:T(8,128)S(1)} %convert_add_fusion.3), channel_id=1, source_target_pairs={{0,8},{8,16},{16,24},{24,32},{32,40},{40,48},{48,56},{56,64},{64,7... | collective-permute-start | bytes 1572872 | tf_op jit(solution)/shard_map/while/body/eval_jaxpr/ppermute | solution.py:13
  178.7 15.3 %collective-permute-start = (bf16[2,512,1,128]{3,1,2,0:T(8,128)(2,1)S(1)}, bf16[2,512,1,128]{3,1,2,0:T(8,128)(2,1)S(1)}, u32[]{:S(2)}, u32[]{:S(2)}) collective-permute-start(bf16[2,512,1,128]{3,1,2,0:T(8,128)(2,1)S(1)} %copy.49), channel_id=1, source_target_pairs={{0,8},{8,16},{16,24},{24,32},{32,40},{40,48},{48,56},{56,64},{64,7... | collective-permute-start | bytes 786440 | tf_op jit(solution)/shard_map/while/body/eval_jaxpr/ppermute | solution.py:13
  198.1 15.4 %collective-permute-start.1 = (f32[2,512,1,128]{3,1,2,0:T(8,128)S(1)}, f32[2,512,1,128]{3,1,2,0:T(8,128)S(1)}, u32[]{:S(2)}, u32[]{:S(2)}) collective-permute-start(f32[2,512,1,128]{3,1,2,0:T(8,128)S(1)} %convert_add_fusion.3), channel_id=1, source_target_pairs={{0,8},{8,16},{16,24},{24,32},{32,40},{40,48},{48,56},{56,64},{64,7... | collective-permute-start | bytes 1572872 | tf_op jit(solution)/shard_map/while/body/eval_jaxpr/ppermute | solution.py:13
  198.2 15.3 %collective-permute-start = (bf16[2,512,1,128]{3,1,2,0:T(8,128)(2,1)S(1)}, bf16[2,512,1,128]{3,1,2,0:T(8,128)(2,1)S(1)}, u32[]{:S(2)}, u32[]{:S(2)}) collective-permute-start(bf16[2,512,1,128]{3,1,2,0:T(8,128)(2,1)S(1)} %copy.49), channel_id=1, source_target_pairs={{0,8},{8,16},{16,24},{24,32},{32,40},{40,48},{48,56},{56,64},{64,7... | collective-permute-start | bytes 786440 | tf_op jit(solution)/shard_map/while/body/eval_jaxpr/ppermute | solution.py:13
  217.6 15.4 %collective-permute-start.1 = (f32[2,512,1,128]{3,1,2,0:T(8,128)S(1)}, f32[2,512,1,128]{3,1,2,0:T(8,128)S(1)}, u32[]{:S(2)}, u32[]{:S(2)}) collective-permute-start(f32[2,512,1,128]{3,1,2,0:T(8,128)S(1)} %convert_add_fusion.3), channel_id=1, source_target_pairs={{0,8},{8,16},{16,24},{24,32},{32,40},{40,48},{48,56},{56,64},{64,7... | collective-permute-start | bytes 1572872 | tf_op jit(solution)/shard_map/while/body/eval_jaxpr/ppermute | solution.py:13
  217.7 15.3 %collective-permute-start = (bf16[2,512,1,128]{3,1,2,0:T(8,128)(2,1)S(1)}, bf16[2,512,1,128]{3,1,2,0:T(8,128)(2,1)S(1)}, u32[]{:S(2)}, u32[]{:S(2)}) collective-permute-start(bf16[2,512,1,128]{3,1,2,0:T(8,128)(2,1)S(1)} %copy.49), channel_id=1, source_target_pairs={{0,8},{8,16},{16,24},{24,32},{32,40},{40,48},{48,56},{56,64},{64,7... | collective-permute-start | bytes 786440 | tf_op jit(solution)/shard_map/while/body/eval_jaxpr/ppermute | solution.py:13
  237.1 15.4 %collective-permute-start.1 = (f32[2,512,1,128]{3,1,2,0:T(8,128)S(1)}, f32[2,512,1,128]{3,1,2,0:T(8,128)S(1)}, u32[]{:S(2)}, u32[]{:S(2)}) collective-permute-start(f32[2,512,1,128]{3,1,2,0:T(8,128)S(1)} %convert_add_fusion.3), channel_id=1, source_target_pairs={{0,8},{8,16},{16,24},{24,32},{32,40},{40,48},{48,56},{56,64},{64,7... | collective-permute-start | bytes 1572872 | tf_op jit(solution)/shard_map/while/body/eval_jaxpr/ppermute | solution.py:13
  237.2 15.3 %collective-permute-start = (bf16[2,512,1,128]{3,1,2,0:T(8,128)(2,1)S(1)}, bf16[2,512,1,128]{3,1,2,0:T(8,128)(2,1)S(1)}, u32[]{:S(2)}, u32[]{:S(2)}) collective-permute-start(bf16[2,512,1,128]{3,1,2,0:T(8,128)(2,1)S(1)} %copy.49), channel_id=1, source_target_pairs={{0,8},{8,16},{16,24},{24,32},{32,40},{40,48},{48,56},{56,64},{64,7... | collective-permute-start | bytes 786440 | tf_op jit(solution)/shard_map/while/body/eval_jaxpr/ppermute | solution.py:13
  256.6 15.4 %collective-permute-start.1 = (f32[2,512,1,128]{3,1,2,0:T(8,128)S(1)}, f32[2,512,1,128]{3,1,2,0:T(8,128)S(1)}, u32[]{:S(2)}, u32[]{:S(2)}) collective-permute-start(f32[2,512,1,128]{3,1,2,0:T(8,128)S(1)} %convert_add_fusion.3), channel_id=1, source_target_pairs={{0,8},{8,16},{16,24},{24,32},{32,40},{40,48},{48,56},{56,64},{64,7... | collective-permute-start | bytes 1572872 | tf_op jit(solution)/shard_map/while/body/eval_jaxpr/ppermute | solution.py:13
  256.7 15.3 %collective-permute-start = (bf16[2,512,1,128]{3,1,2,0:T(8,128)(2,1)S(1)}, bf16[2,512,1,128]{3,1,2,0:T(8,128)(2,1)S(1)}, u32[]{:S(2)}, u32[]{:S(2)}) collective-permute-start(bf16[2,512,1,128]{3,1,2,0:T(8,128)(2,1)S(1)} %copy.49), channel_id=1, source_target_pairs={{0,8},{8,16},{16,24},{24,32},{32,40},{40,48},{48,56},{56,64},{64,7... | collective-permute-start | bytes 786440 | tf_op jit(solution)/shard_map/while/body/eval_jaxpr/ppermute | solution.py:13
  276.1 15.4 %collective-permute-start.1 = (f32[2,512,1,128]{3,1,2,0:T(8,128)S(1)}, f32[2,512,1,128]{3,1,2,0:T(8,128)S(1)}, u32[]{:S(2)}, u32[]{:S(2)}) collective-permute-start(f32[2,512,1,128]{3,1,2,0:T(8,128)S(1)} %convert_add_fusion.3), channel_id=1, source_target_pairs={{0,8},{8,16},{16,24},{24,32},{32,40},{40,48},{48,56},{56,64},{64,7... | collective-permute-start | bytes 1572872 | tf_op jit(solution)/shard_map/while/body/eval_jaxpr/ppermute | solution.py:13
  276.2 15.3 %collective-permute-start = (bf16[2,512,1,128]{3,1,2,0:T(8,128)(2,1)S(1)}, bf16[2,512,1,128]{3,1,2,0:T(8,128)(2,1)S(1)}, u32[]{:S(2)}, u32[]{:S(2)}) collective-permute-start(bf16[2,512,1,128]{3,1,2,0:T(8,128)(2,1)S(1)} %copy.49), channel_id=1, source_target_pairs={{0,8},{8,16},{16,24},{24,32},{32,40},{40,48},{48,56},{56,64},{64,7... | collective-permute-start | bytes 786440 | tf_op jit(solution)/shard_map/while/body/eval_jaxpr/ppermute | solution.py:13
  295.5 15.4 %collective-permute-start.1 = (f32[2,512,1,128]{3,1,2,0:T(8,128)S(1)}, f32[2,512,1,128]{3,1,2,0:T(8,128)S(1)}, u32[]{:S(2)}, u32[]{:S(2)}) collective-permute-start(f32[2,512,1,128]{3,1,2,0:T(8,128)S(1)} %convert_add_fusion.3), channel_id=1, source_target_pairs={{0,8},{8,16},{16,24},{24,32},{32,40},{40,48},{48,56},{56,64},{64,7... | collective-permute-start | bytes 1572872 | tf_op jit(solution)/shard_map/while/body/eval_jaxpr/ppermute | solution.py:13
  295.6 15.3 %collective-permute-start = (bf16[2,512,1,128]{3,1,2,0:T(8,128)(2,1)S(1)}, bf16[2,512,1,128]{3,1,2,0:T(8,128)(2,1)S(1)}, u32[]{:S(2)}, u32[]{:S(2)}) collective-permute-start(bf16[2,512,1,128]{3,1,2,0:T(8,128)(2,1)S(1)} %copy.49), channel_id=1, source_target_pairs={{0,8},{8,16},{16,24},{24,32},{32,40},{40,48},{48,56},{56,64},{64,7... | collective-permute-start | bytes 786440 | tf_op jit(solution)/shard_map/while/body/eval_jaxpr/ppermute | solution.py:13
  315.0 15.4 %collective-permute-start.1 = (f32[2,512,1,128]{3,1,2,0:T(8,128)S(1)}, f32[2,512,1,128]{3,1,2,0:T(8,128)S(1)}, u32[]{:S(2)}, u32[]{:S(2)}) collective-permute-start(f32[2,512,1,128]{3,1,2,0:T(8,128)S(1)} %convert_add_fusion.3), channel_id=1, source_target_pairs={{0,8},{8,16},{16,24},{24,32},{32,40},{40,48},{48,56},{56,64},{64,7... | collective-permute-start | bytes 1572872 | tf_op jit(solution)/shard_map/while/body/eval_jaxpr/ppermute | solution.py:13
  315.1 15.3 %collective-permute-start = (bf16[2,512,1,128]{3,1,2,0:T(8,128)(2,1)S(1)}, bf16[2,512,1,128]{3,1,2,0:T(8,128)(2,1)S(1)}, u32[]{:S(2)}, u32[]{:S(2)}) collective-permute-start(bf16[2,512,1,128]{3,1,2,0:T(8,128)(2,1)S(1)} %copy.49), channel_id=1, source_target_pairs={{0,8},{8,16},{16,24},{24,32},{32,40},{40,48},{48,56},{56,64},{64,7... | collective-permute-start | bytes 786440 | tf_op jit(solution)/shard_map/while/body/eval_jaxpr/ppermute | solution.py:13
  334.5 15.4 %collective-permute-start.1 = (f32[2,512,1,128]{3,1,2,0:T(8,128)S(1)}, f32[2,512,1,128]{3,1,2,0:T(8,128)S(1)}, u32[]{:S(2)}, u32[]{:S(2)}) collective-permute-start(f32[2,512,1,128]{3,1,2,0:T(8,128)S(1)} %convert_add_fusion.3), channel_id=1, source_target_pairs={{0,8},{8,16},{16,24},{24,32},{32,40},{40,48},{48,56},{56,64},{64,7... | collective-permute-start | bytes 1572872 | tf_op jit(solution)/shard_map/while/body/eval_jaxpr/ppermute | solution.py:13
  334.6 15.3 %collective-permute-start = (bf16[2,512,1,128]{3,1,2,0:T(8,128)(2,1)S(1)}, bf16[2,512,1,128]{3,1,2,0:T(8,128)(2,1)S(1)}, u32[]{:S(2)}, u32[]{:S(2)}) collective-permute-start(bf16[2,512,1,128]{3,1,2,0:T(8,128)(2,1)S(1)} %copy.49), channel_id=1, source_target_pairs={{0,8},{8,16},{16,24},{24,32},{32,40},{40,48},{48,56},{56,64},{64,7... | collective-permute-start | bytes 786440 | tf_op jit(solution)/shard_map/while/body/eval_jaxpr/ppermute | solution.py:13
  354.0 15.4 %collective-permute-start.1 = (f32[2,512,1,128]{3,1,2,0:T(8,128)S(1)}, f32[2,512,1,128]{3,1,2,0:T(8,128)S(1)}, u32[]{:S(2)}, u32[]{:S(2)}) collective-permute-start(f32[2,512,1,128]{3,1,2,0:T(8,128)S(1)} %convert_add_fusion.3), channel_id=1, source_target_pairs={{0,8},{8,16},{16,24},{24,32},{32,40},{40,48},{48,56},{56,64},{64,7... | collective-permute-start | bytes 1572872 | tf_op jit(solution)/shard_map/while/body/eval_jaxpr/ppermute | solution.py:13
  354.1 15.3 %collective-permute-start = (bf16[2,512,1,128]{3,1,2,0:T(8,128)(2,1)S(1)}, bf16[2,512,1,128]{3,1,2,0:T(8,128)(2,1)S(1)}, u32[]{:S(2)}, u32[]{:S(2)}) collective-permute-start(bf16[2,512,1,128]{3,1,2,0:T(8,128)(2,1)S(1)} %copy.49), channel_id=1, source_target_pairs={{0,8},{8,16},{16,24},{24,32},{32,40},{40,48},{48,56},{56,64},{64,7... | collective-permute-start | bytes 786440 | tf_op jit(solution)/shard_map/while/body/eval_jaxpr/ppermute | solution.py:13
  373.5 15.4 %collective-permute-start.1 = (f32[2,512,1,128]{3,1,2,0:T(8,128)S(1)}, f32[2,512,1,128]{3,1,2,0:T(8,128)S(1)}, u32[]{:S(2)}, u32[]{:S(2)}) collective-permute-start(f32[2,512,1,128]{3,1,2,0:T(8,128)S(1)} %convert_add_fusion.3), channel_id=1, source_target_pairs={{0,8},{8,16},{16,24},{24,32},{32,40},{40,48},{48,56},{56,64},{64,7... | collective-permute-start | bytes 1572872 | tf_op jit(solution)/shard_map/while/body/eval_jaxpr/ppermute | solution.py:13
  373.6 15.3 %collective-permute-start = (bf16[2,512,1,128]{3,1,2,0:T(8,128)(2,1)S(1)}, bf16[2,512,1,128]{3,1,2,0:T(8,128)(2,1)S(1)}, u32[]{:S(2)}, u32[]{:S(2)}) collective-permute-start(bf16[2,512,1,128]{3,1,2,0:T(8,128)(2,1)S(1)} %copy.49), channel_id=1, source_target_pairs={{0,8},{8,16},{16,24},{24,32},{32,40},{40,48},{48,56},{56,64},{64,7... | collective-permute-start | bytes 786440 | tf_op jit(solution)/shard_map/while/body/eval_jaxpr/ppermute | solution.py:13
  393.0 15.4 %collective-permute-start.1 = (f32[2,512,1,128]{3,1,2,0:T(8,128)S(1)}, f32[2,512,1,128]{3,1,2,0:T(8,128)S(1)}, u32[]{:S(2)}, u32[]{:S(2)}) collective-permute-start(f32[2,512,1,128]{3,1,2,0:T(8,128)S(1)} %convert_add_fusion.3), channel_id=1, source_target_pairs={{0,8},{8,16},{16,24},{24,32},{32,40},{40,48},{48,56},{56,64},{64,7... | collective-permute-start | bytes 1572872 | tf_op jit(solution)/shard_map/while/body/eval_jaxpr/ppermute | solution.py:13
  393.0 15.3 %collective-permute-start = (bf16[2,512,1,128]{3,1,2,0:T(8,128)(2,1)S(1)}, bf16[2,512,1,128]{3,1,2,0:T(8,128)(2,1)S(1)}, u32[]{:S(2)}, u32[]{:S(2)}) collective-permute-start(bf16[2,512,1,128]{3,1,2,0:T(8,128)(2,1)S(1)} %copy.49), channel_id=1, source_target_pairs={{0,8},{8,16},{16,24},{24,32},{32,40},{40,48},{48,56},{56,64},{64,7... | collective-permute-start | bytes 786440 | tf_op jit(solution)/shard_map/while/body/eval_jaxpr/ppermute | solution.py:13
  412.4 15.4 %collective-permute-start.1 = (f32[2,512,1,128]{3,1,2,0:T(8,128)S(1)}, f32[2,512,1,128]{3,1,2,0:T(8,128)S(1)}, u32[]{:S(2)}, u32[]{:S(2)}) collective-permute-start(f32[2,512,1,128]{3,1,2,0:T(8,128)S(1)} %convert_add_fusion.3), channel_id=1, source_target_pairs={{0,8},{8,16},{16,24},{24,32},{32,40},{40,48},{48,56},{56,64},{64,7... | collective-permute-start | bytes 1572872 | tf_op jit(solution)/shard_map/while/body/eval_jaxpr/ppermute | solution.py:13
  412.5 15.3 %collective-permute-start = (bf16[2,512,1,128]{3,1,2,0:T(8,128)(2,1)S(1)}, bf16[2,512,1,128]{3,1,2,0:T(8,128)(2,1)S(1)}, u32[]{:S(2)}, u32[]{:S(2)}) collective-permute-start(bf16[2,512,1,128]{3,1,2,0:T(8,128)(2,1)S(1)} %copy.49), channel_id=1, source_target_pairs={{0,8},{8,16},{16,24},{24,32},{32,40},{40,48},{48,56},{56,64},{64,7... | collective-permute-start | bytes 786440 | tf_op jit(solution)/shard_map/while/body/eval_jaxpr/ppermute | solution.py:13
  431.9 15.4 %collective-permute-start.1 = (f32[2,512,1,128]{3,1,2,0:T(8,128)S(1)}, f32[2,512,1,128]{3,1,2,0:T(8,128)S(1)}, u32[]{:S(2)}, u32[]{:S(2)}) collective-permute-start(f32[2,512,1,128]{3,1,2,0:T(8,128)S(1)} %convert_add_fusion.3), channel_id=1, source_target_pairs={{0,8},{8,16},{16,24},{24,32},{32,40},{40,48},{48,56},{56,64},{64,7... | collective-permute-start | bytes 1572872 | tf_op jit(solution)/shard_map/while/body/eval_jaxpr/ppermute | solution.py:13
  432.0 15.3 %collective-permute-start = (bf16[2,512,1,128]{3,1,2,0:T(8,128)(2,1)S(1)}, bf16[2,512,1,128]{3,1,2,0:T(8,128)(2,1)S(1)}, u32[]{:S(2)}, u32[]{:S(2)}) collective-permute-start(bf16[2,512,1,128]{3,1,2,0:T(8,128)(2,1)S(1)} %copy.49), channel_id=1, source_target_pairs={{0,8},{8,16},{16,24},{24,32},{32,40},{40,48},{48,56},{56,64},{64,7... | collective-permute-start | bytes 786440 | tf_op jit(solution)/shard_map/while/body/eval_jaxpr/ppermute | solution.py:13
  451.4 15.4 %collective-permute-start.1 = (f32[2,512,1,128]{3,1,2,0:T(8,128)S(1)}, f32[2,512,1,128]{3,1,2,0:T(8,128)S(1)}, u32[]{:S(2)}, u32[]{:S(2)}) collective-permute-start(f32[2,512,1,128]{3,1,2,0:T(8,128)S(1)} %convert_add_fusion.3), channel_id=1, source_target_pairs={{0,8},{8,16},{16,24},{24,32},{32,40},{40,48},{48,56},{56,64},{64,7... | collective-permute-start | bytes 1572872 | tf_op jit(solution)/shard_map/while/body/eval_jaxpr/ppermute | solution.py:13
  451.5 15.3 %collective-permute-start = (bf16[2,512,1,128]{3,1,2,0:T(8,128)(2,1)S(1)}, bf16[2,512,1,128]{3,1,2,0:T(8,128)(2,1)S(1)}, u32[]{:S(2)}, u32[]{:S(2)}) collective-permute-start(bf16[2,512,1,128]{3,1,2,0:T(8,128)(2,1)S(1)} %copy.49), channel_id=1, source_target_pairs={{0,8},{8,16},{16,24},{24,32},{32,40},{40,48},{48,56},{56,64},{64,7... | collective-permute-start | bytes 786440 | tf_op jit(solution)/shard_map/while/body/eval_jaxpr/ppermute | solution.py:13
  470.9 15.4 %collective-permute-start.1 = (f32[2,512,1,128]{3,1,2,0:T(8,128)S(1)}, f32[2,512,1,128]{3,1,2,0:T(8,128)S(1)}, u32[]{:S(2)}, u32[]{:S(2)}) collective-permute-start(f32[2,512,1,128]{3,1,2,0:T(8,128)S(1)} %convert_add_fusion.3), channel_id=1, source_target_pairs={{0,8},{8,16},{16,24},{24,32},{32,40},{40,48},{48,56},{56,64},{64,7... | collective-permute-start | bytes 1572872 | tf_op jit(solution)/shard_map/while/body/eval_jaxpr/ppermute | solution.py:13
  471.0 15.3 %collective-permute-start = (bf16[2,512,1,128]{3,1,2,0:T(8,128)(2,1)S(1)}, bf16[2,512,1,128]{3,1,2,0:T(8,128)(2,1)S(1)}, u32[]{:S(2)}, u32[]{:S(2)}) collective-permute-start(bf16[2,512,1,128]{3,1,2,0:T(8,128)(2,1)S(1)} %copy.49), channel_id=1, source_target_pairs={{0,8},{8,16},{16,24},{24,32},{32,40},{40,48},{48,56},{56,64},{64,7... | collective-permute-start | bytes 786440 | tf_op jit(solution)/shard_map/while/body/eval_jaxpr/ppermute | solution.py:13
  490.4 15.4 %collective-permute-start.1 = (f32[2,512,1,128]{3,1,2,0:T(8,128)S(1)}, f32[2,512,1,128]{3,1,2,0:T(8,128)S(1)}, u32[]{:S(2)}, u32[]{:S(2)}) collective-permute-start(f32[2,512,1,128]{3,1,2,0:T(8,128)S(1)} %convert_add_fusion.3), channel_id=1, source_target_pairs={{0,8},{8,16},{16,24},{24,32},{32,40},{40,48},{48,56},{56,64},{64,7... | collective-permute-start | bytes 1572872 | tf_op jit(solution)/shard_map/while/body/eval_jaxpr/ppermute | solution.py:13
  490.5 15.3 %collective-permute-start = (bf16[2,512,1,128]{3,1,2,0:T(8,128)(2,1)S(1)}, bf16[2,512,1,128]{3,1,2,0:T(8,128)(2,1)S(1)}, u32[]{:S(2)}, u32[]{:S(2)}) collective-permute-start(bf16[2,512,1,128]{3,1,2,0:T(8,128)(2,1)S(1)} %copy.49), channel_id=1, source_target_pairs={{0,8},{8,16},{16,24},{24,32},{32,40},{40,48},{48,56},{56,64},{64,7... | collective-permute-start | bytes 786440 | tf_op jit(solution)/shard_map/while/body/eval_jaxpr/ppermute | solution.py:13
  509.8 15.4 %collective-permute-start.1 = (f32[2,512,1,128]{3,1,2,0:T(8,128)S(1)}, f32[2,512,1,128]{3,1,2,0:T(8,128)S(1)}, u32[]{:S(2)}, u32[]{:S(2)}) collective-permute-start(f32[2,512,1,128]{3,1,2,0:T(8,128)S(1)} %convert_add_fusion.3), channel_id=1, source_target_pairs={{0,8},{8,16},{16,24},{24,32},{32,40},{40,48},{48,56},{56,64},{64,7... | collective-permute-start | bytes 1572872 | tf_op jit(solution)/shard_map/while/body/eval_jaxpr/ppermute | solution.py:13
  509.9 15.3 %collective-permute-start = (bf16[2,512,1,128]{3,1,2,0:T(8,128)(2,1)S(1)}, bf16[2,512,1,128]{3,1,2,0:T(8,128)(2,1)S(1)}, u32[]{:S(2)}, u32[]{:S(2)}) collective-permute-start(bf16[2,512,1,128]{3,1,2,0:T(8,128)(2,1)S(1)} %copy.49), channel_id=1, source_target_pairs={{0,8},{8,16},{16,24},{24,32},{32,40},{40,48},{48,56},{56,64},{64,7... | collective-permute-start | bytes 786440 | tf_op jit(solution)/shard_map/while/body/eval_jaxpr/ppermute | solution.py:13
  529.3 15.4 %collective-permute-start.1 = (f32[2,512,1,128]{3,1,2,0:T(8,128)S(1)}, f32[2,512,1,128]{3,1,2,0:T(8,128)S(1)}, u32[]{:S(2)}, u32[]{:S(2)}) collective-permute-start(f32[2,512,1,128]{3,1,2,0:T(8,128)S(1)} %convert_add_fusion.3), channel_id=1, source_target_pairs={{0,8},{8,16},{16,24},{24,32},{32,40},{40,48},{48,56},{56,64},{64,7... | collective-permute-start | bytes 1572872 | tf_op jit(solution)/shard_map/while/body/eval_jaxpr/ppermute | solution.py:13
  529.4 15.3 %collective-permute-start = (bf16[2,512,1,128]{3,1,2,0:T(8,128)(2,1)S(1)}, bf16[2,512,1,128]{3,1,2,0:T(8,128)(2,1)S(1)}, u32[]{:S(2)}, u32[]{:S(2)}) collective-permute-start(bf16[2,512,1,128]{3,1,2,0:T(8,128)(2,1)S(1)} %copy.49), channel_id=1, source_target_pairs={{0,8},{8,16},{16,24},{24,32},{32,40},{40,48},{48,56},{56,64},{64,7... | collective-permute-start | bytes 786440 | tf_op jit(solution)/shard_map/while/body/eval_jaxpr/ppermute | solution.py:13
  548.8 15.4 %collective-permute-start.1 = (f32[2,512,1,128]{3,1,2,0:T(8,128)S(1)}, f32[2,512,1,128]{3,1,2,0:T(8,128)S(1)}, u32[]{:S(2)}, u32[]{:S(2)}) collective-permute-start(f32[2,512,1,128]{3,1,2,0:T(8,128)S(1)} %convert_add_fusion.3), channel_id=1, source_target_pairs={{0,8},{8,16},{16,24},{24,32},{32,40},{40,48},{48,56},{56,64},{64,7... | collective-permute-start | bytes 1572872 | tf_op jit(solution)/shard_map/while/body/eval_jaxpr/ppermute | solution.py:13
  548.9 15.3 %collective-permute-start = (bf16[2,512,1,128]{3,1,2,0:T(8,128)(2,1)S(1)}, bf16[2,512,1,128]{3,1,2,0:T(8,128)(2,1)S(1)}, u32[]{:S(2)}, u32[]{:S(2)}) collective-permute-start(bf16[2,512,1,128]{3,1,2,0:T(8,128)(2,1)S(1)} %copy.49), channel_id=1, source_target_pairs={{0,8},{8,16},{16,24},{24,32},{32,40},{40,48},{48,56},{56,64},{64,7... | collective-permute-start | bytes 786440 | tf_op jit(solution)/shard_map/while/body/eval_jaxpr/ppermute | solution.py:13
  568.3 15.4 %collective-permute-start.1 = (f32[2,512,1,128]{3,1,2,0:T(8,128)S(1)}, f32[2,512,1,128]{3,1,2,0:T(8,128)S(1)}, u32[]{:S(2)}, u32[]{:S(2)}) collective-permute-start(f32[2,512,1,128]{3,1,2,0:T(8,128)S(1)} %convert_add_fusion.3), channel_id=1, source_target_pairs={{0,8},{8,16},{16,24},{24,32},{32,40},{40,48},{48,56},{56,64},{64,7... | collective-permute-start | bytes 1572872 | tf_op jit(solution)/shard_map/while/body/eval_jaxpr/ppermute | solution.py:13
  568.4 15.3 %collective-permute-start = (bf16[2,512,1,128]{3,1,2,0:T(8,128)(2,1)S(1)}, bf16[2,512,1,128]{3,1,2,0:T(8,128)(2,1)S(1)}, u32[]{:S(2)}, u32[]{:S(2)}) collective-permute-start(bf16[2,512,1,128]{3,1,2,0:T(8,128)(2,1)S(1)} %copy.49), channel_id=1, source_target_pairs={{0,8},{8,16},{16,24},{24,32},{32,40},{40,48},{48,56},{56,64},{64,7... | collective-permute-start | bytes 786440 | tf_op jit(solution)/shard_map/while/body/eval_jaxpr/ppermute | solution.py:13
  587.8 15.4 %collective-permute-start.1 = (f32[2,512,1,128]{3,1,2,0:T(8,128)S(1)}, f32[2,512,1,128]{3,1,2,0:T(8,128)S(1)}, u32[]{:S(2)}, u32[]{:S(2)}) collective-permute-start(f32[2,512,1,128]{3,1,2,0:T(8,128)S(1)} %convert_add_fusion.3), channel_id=1, source_target_pairs={{0,8},{8,16},{16,24},{24,32},{32,40},{40,48},{48,56},{56,64},{64,7... | collective-permute-start | bytes 1572872 | tf_op jit(solution)/shard_map/while/body/eval_jaxpr/ppermute | solution.py:13
  587.9 15.3 %collective-permute-start = (bf16[2,512,1,128]{3,1,2,0:T(8,128)(2,1)S(1)}, bf16[2,512,1,128]{3,1,2,0:T(8,128)(2,1)S(1)}, u32[]{:S(2)}, u32[]{:S(2)}) collective-permute-start(bf16[2,512,1,128]{3,1,2,0:T(8,128)(2,1)S(1)} %copy.49), channel_id=1, source_target_pairs={{0,8},{8,16},{16,24},{24,32},{32,40},{40,48},{48,56},{56,64},{64,7... | collective-permute-start | bytes 786440 | tf_op jit(solution)/shard_map/while/body/eval_jaxpr/ppermute | solution.py:13
  607.3 15.4 %collective-permute-start.1 = (f32[2,512,1,128]{3,1,2,0:T(8,128)S(1)}, f32[2,512,1,128]{3,1,2,0:T(8,128)S(1)}, u32[]{:S(2)}, u32[]{:S(2)}) collective-permute-start(f32[2,512,1,128]{3,1,2,0:T(8,128)S(1)} %convert_add_fusion.3), channel_id=1, source_target_pairs={{0,8},{8,16},{16,24},{24,32},{32,40},{40,48},{48,56},{56,64},{64,7... | collective-permute-start | bytes 1572872 | tf_op jit(solution)/shard_map/while/body/eval_jaxpr/ppermute | solution.py:13
  607.4 15.3 %collective-permute-start = (bf16[2,512,1,128]{3,1,2,0:T(8,128)(2,1)S(1)}, bf16[2,512,1,128]{3,1,2,0:T(8,128)(2,1)S(1)}, u32[]{:S(2)}, u32[]{:S(2)}) collective-permute-start(bf16[2,512,1,128]{3,1,2,0:T(8,128)(2,1)S(1)} %copy.49), channel_id=1, source_target_pairs={{0,8},{8,16},{16,24},{24,32},{32,40},{40,48},{48,56},{56,64},{64,7... | collective-permute-start | bytes 786440 | tf_op jit(solution)/shard_map/while/body/eval_jaxpr/ppermute | solution.py:13
  626.7 15.4 %collective-permute-start.1 = (f32[2,512,1,128]{3,1,2,0:T(8,128)S(1)}, f32[2,512,1,128]{3,1,2,0:T(8,128)S(1)}, u32[]{:S(2)}, u32[]{:S(2)}) collective-permute-start(f32[2,512,1,128]{3,1,2,0:T(8,128)S(1)} %convert_add_fusion.3), channel_id=1, source_target_pairs={{0,8},{8,16},{16,24},{24,32},{32,40},{40,48},{48,56},{56,64},{64,7... | collective-permute-start | bytes 1572872 | tf_op jit(solution)/shard_map/while/body/eval_jaxpr/ppermute | solution.py:13
  626.8 15.3 %collective-permute-start = (bf16[2,512,1,128]{3,1,2,0:T(8,128)(2,1)S(1)}, bf16[2,512,1,128]{3,1,2,0:T(8,128)(2,1)S(1)}, u32[]{:S(2)}, u32[]{:S(2)}) collective-permute-start(bf16[2,512,1,128]{3,1,2,0:T(8,128)(2,1)S(1)} %copy.49), channel_id=1, source_target_pairs={{0,8},{8,16},{16,24},{24,32},{32,40},{40,48},{48,56},{56,64},{64,7... | collective-permute-start | bytes 786440 | tf_op jit(solution)/shard_map/while/body/eval_jaxpr/ppermute | solution.py:13
  646.2 15.4 %collective-permute-start.1 = (f32[2,512,1,128]{3,1,2,0:T(8,128)S(1)}, f32[2,512,1,128]{3,1,2,0:T(8,128)S(1)}, u32[]{:S(2)}, u32[]{:S(2)}) collective-permute-start(f32[2,512,1,128]{3,1,2,0:T(8,128)S(1)} %convert_add_fusion.3), channel_id=1, source_target_pairs={{0,8},{8,16},{16,24},{24,32},{32,40},{40,48},{48,56},{56,64},{64,7... | collective-permute-start | bytes 1572872 | tf_op jit(solution)/shard_map/while/body/eval_jaxpr/ppermute | solution.py:13
  646.3 15.3 %collective-permute-start = (bf16[2,512,1,128]{3,1,2,0:T(8,128)(2,1)S(1)}, bf16[2,512,1,128]{3,1,2,0:T(8,128)(2,1)S(1)}, u32[]{:S(2)}, u32[]{:S(2)}) collective-permute-start(bf16[2,512,1,128]{3,1,2,0:T(8,128)(2,1)S(1)} %copy.49), channel_id=1, source_target_pairs={{0,8},{8,16},{16,24},{24,32},{32,40},{40,48},{48,56},{56,64},{64,7... | collective-permute-start | bytes 786440 | tf_op jit(solution)/shard_map/while/body/eval_jaxpr/ppermute | solution.py:13
  (7 other events, 833.9 us)
Sparse Core Ops, SparseCore 0:
  9.8 64.3 all-gather.1
  675.3 106.6 reduce-scatter.1
where the time goes:
time: 792 us; the launch traced here: 790 us
  waiting for transfers between devices  612 us (77%)
  local copies, waits for them, and re-layouts  79.1 us (10%)
  matrix products  63.9 us (8%)
  between operations  13.6 us (2%)
  starting transfers between devices  13.3 us (2%)
    ppermute x63, waiting for transfers between devices, from_behind(): lax.ppermute(value, axis, [(i, (i + by) % count) for i in range(count)])  442 us
    reduce_scatter x1, waiting for transfers between devices, per_device(): lax.psum_scatter(total + lax.dot_general(w_value, d_value, contract, pref...  107 us
    all_gather x1, waiting for transfers between devices, per_device(): lax.all_gather(out_grad, 'head', axis=1, tiled=True)  61.9 us
    broadcast_in_dim x31, local copies, waits for them, and re-layouts, visit(): jnp.repeat(jnp.repeat(listed, TILE, axis=0), TILE, axis=1)  49.5 us
    dynamic_slice x32, local copies, waits for them, and re-layouts, visit(): lax.dynamic_slice_in_dim(trace_id, first_tile * TILE, key_block.shape[0], 0)  24.4 us
  transfers between devices with their start and end apart: 65, of which 34 were waited for; matrix products, arithmetic and copies ran while one was open for 2% of the time, Pallas kernels for 0%

commit v1 on v0

--- a/solution.py
+++ b/solution.py
@@ -62,7 +62,9 @@
     seq_index = lax.axis_index("seq")
     tiles_here = tokens_here // TILE
     d_attn = lax.dot_general(
-        lax.all_gather(out_grad, "head", axis=1, tiled=True),
+        jnp.concatenate(
+            lax.all_to_all(jnp.stack([out_grad] * lax.axis_size("head")), "head", 0, 0), axis=1
+        ),
         w_out,
         (((1,), (1,)), ((), ())),
         preferred_element_type=jnp.float32,

time: 792 us -> 763 us (0.963)
  waiting for transfers between devices: 612 us -> 574 us
  starting transfers between devices: 13.3 us -> 24.8 us
    all_gather x1 -> x0, waiting for transfers between devices: 61.9 us -> none  [per_device(): lax.all_gather(out_grad, 'head', axis=1, tiled=True)]
    all_to_all x0 -> x1, waiting for transfers between devices: none -> 20.1 us  [per_device(): lax.all_to_all(jnp.stack([out_grad] * lax.axis_size('head')), 'head', 0, 0)]
    all_to_all x0 -> x1, starting transfers between devices: none -> 10.9 us  [per_device(): lax.all_to_all(jnp.stack([out_grad] * lax.axis_size('head')), 'head', 0, 0)]
where the time goes in v1:
time: 763 us; the launch traced here: 761 us
  waiting for transfers between devices  574 us (75%)
  local copies, waits for them, and re-layouts  80.4 us (11%)
  matrix products  62.5 us (8%)
  starting transfers between devices  24.8 us (3%)
  between operations  13.7 us (2%)
    ppermute x63, waiting for transfers between devices, from_behind(): lax.ppermute(value, axis, [(i, (i + by) % count) for i in range(count)])  442 us
    reduce_scatter x1, waiting for transfers between devices, per_device(): lax.psum_scatter(total + lax.dot_general(w_value, d_value, contract, pref...  112 us
    broadcast_in_dim x31, local copies, waits for them, and re-layouts, visit(): jnp.repeat(jnp.repeat(listed, TILE, axis=0), TILE, axis=1)  49.5 us
    dynamic_slice x32, local copies, waits for them, and re-layouts, visit(): lax.dynamic_slice_in_dim(trace_id, first_tile * TILE, key_block.shape[0], 0)  24.4 us
    all_to_all x1, waiting for transfers between devices, per_device(): lax.all_to_all(jnp.stack([out_grad] * lax.axis_size('head')), 'head', 0, 0)  20.1 us
    dot_general x32, matrix products, pair_grads(): jnp.einsum('rhd,chd->hrc', query_heads, key_heads, preferred_element_type...  15.7 us
  transfers between devices with their start and end apart: 65, of which 34 were waited for; matrix products, arithmetic and copies ran while one was open for 2% of the time, Pallas kernels for 0%

profile of v1, /device:TPU:8, one launch (start us, length us, event | category | flops | bytes accessed | tf_op | source)
XLA Modules:
  0.0 761.5 jit_solution(18106558988705984346)
XLA Ops:
  8.7 10.9 %all-to-all-start = ((bf16[8,512,128]{1,2,0:T(8,128)(2,1)}), bf16[8,512,128]{1,2,0:T(8,128)(2,1)S(1)}, u32[]{:S(2)}, u32[]{:S(2)}) async-start(bf16[8,512,128]{1,2,0:T(8,128)(2,1)} %stack.68), calls=%async_computation | async-start | bytes 2097152 | tf_op jit(solution)/shard_map/all_to_all | solution.py:66
  21.5 20.1 %all-to-all-done = bf16[8,512,128]{1,2,0:T(8,128)(2,1)S(1)} async-done(((bf16[8,512,128]{1,2,0:T(8,128)(2,1)}), bf16[8,512,128]{1,2,0:T(8,128)(2,1)S(1)}, u32[]{:S(2)}, u32[]{:S(2)}) %all-to-all-start) | async-done | bytes 1048608 | tf_op jit(solution)/shard_map/all_to_all | solution.py:66
  42.1 585.4 %while.20 = (s32[]{:T(128)}, bf16[2,512,1,128]{3,1,2,0:T(8,128)(2,1)S(1)}, f32[2,512,1,128]{3,1,2,0:T(8,128)S(1)}, f32[512,1,128]{2,0,1:T(8,128)S(1)}, s32[]{:T(...) while((s32[]{:T(128)}, ...), condition=%wide.region_3.4_spmd.clone, body=%wide.region_2.3_spmd.clone.sunk | while | flops 338821152 | bytes 11944476 | solution.py:115
  46.3 1.7 collective-permute-start
  48.3 9.4 %collective-permute-done = bf16[2,512,1,128]{3,1,2,0:T(8,128)(2,1)S(1)} collective-permute-done((bf16[2,512,1,128]{3,1,2,0:T(8,128)(2,1)S(1)}, bf16[2,512,1,128]{3,1,2,0:T(8,128)(2,1)S(1)}, u32[]{:S(2)}, u32[]{:S(2)}) %collective-permute-start) | collective-permute-done | bytes 262176 | tf_op jit(solution)/shard_map/while/body/eval_jaxpr/ppermute | solution.py:13
  58.6 1.6 broadcast_in_dim.75
  61.9 1.7 collective-permute-start
  63.9 9.4 %collective-permute-done = bf16[2,512,1,128]{3,1,2,0:T(8,128)(2,1)S(1)} collective-permute-done((bf16[2,512,1,128]{3,1,2,0:T(8,128)(2,1)S(1)}, bf16[2,512,1,128]{3,1,2,0:T(8,128)(2,1)S(1)}, u32[]{:S(2)}, u32[]{:S(2)}) %collective-permute-start) | collective-permute-done | bytes 262176 | tf_op jit(solution)/shard_map/while/body/eval_jaxpr/ppermute | solution.py:13
  74.2 1.6 broadcast_in_dim.75
  77.5 1.7 collective-permute-start
  79.5 9.4 %collective-permute-done = bf16[2,512,1,128]{3,1,2,0:T(8,128)(2,1)S(1)} collective-permute-done((bf16[2,512,1,128]{3,1,2,0:T(8,128)(2,1)S(1)}, bf16[2,512,1,128]{3,1,2,0:T(8,128)(2,1)S(1)}, u32[]{:S(2)}, u32[]{:S(2)}) %collective-permute-start) | collective-permute-done | bytes 262176 | tf_op jit(solution)/shard_map/while/body/eval_jaxpr/ppermute | solution.py:13
  89.8 1.6 broadcast_in_dim.75
  93.1 1.7 collective-permute-start
  95.1 9.4 %collective-permute-done = bf16[2,512,1,128]{3,1,2,0:T(8,128)(2,1)S(1)} collective-permute-done((bf16[2,512,1,128]{3,1,2,0:T(8,128)(2,1)S(1)}, bf16[2,512,1,128]{3,1,2,0:T(8,128)(2,1)S(1)}, u32[]{:S(2)}, u32[]{:S(2)}) %collective-permute-start) | collective-permute-done | bytes 262176 | tf_op jit(solution)/shard_map/while/body/eval_jaxpr/ppermute | solution.py:13
  105.4 1.6 broadcast_in_dim.75
  108.6 1.7 collective-permute-start
  110.6 10.3 %collective-permute-done = bf16[2,512,1,128]{3,1,2,0:T(8,128)(2,1)S(1)} collective-permute-done((bf16[2,512,1,128]{3,1,2,0:T(8,128)(2,1)S(1)}, bf16[2,512,1,128]{3,1,2,0:T(8,128)(2,1)S(1)}, u32[]{:S(2)}, u32[]{:S(2)}) %collective-permute-start) | collective-permute-done | bytes 262176 | tf_op jit(solution)/shard_map/while/body/eval_jaxpr/ppermute | solution.py:13
  121.8 1.6 broadcast_in_dim.75
  126.2 14.2 %collective-permute-done = bf16[2,512,1,128]{3,1,2,0:T(8,128)(2,1)S(1)} collective-permute-done((bf16[2,512,1,128]{3,1,2,0:T(8,128)(2,1)S(1)}, bf16[2,512,1,128]{3,1,2,0:T(8,128)(2,1)S(1)}, u32[]{:S(2)}, u32[]{:S(2)}) %collective-permute-start) | collective-permute-done | bytes 262176 | tf_op jit(solution)/shard_map/while/body/eval_jaxpr/ppermute | solution.py:13
  141.3 1.6 broadcast_in_dim.75
  145.0 14.9 %collective-permute-done = bf16[2,512,1,128]{3,1,2,0:T(8,128)(2,1)S(1)} collective-permute-done((bf16[2,512,1,128]{3,1,2,0:T(8,128)(2,1)S(1)}, bf16[2,512,1,128]{3,1,2,0:T(8,128)(2,1)S(1)}, u32[]{:S(2)}, u32[]{:S(2)}) %collective-permute-start) | collective-permute-done | bytes 262176 | tf_op jit(solution)/shard_map/while/body/eval_jaxpr/ppermute | solution.py:13
  164.5 14.9 %collective-permute-done = bf16[2,512,1,128]{3,1,2,0:T(8,128)(2,1)S(1)} collective-permute-done((bf16[2,512,1,128]{3,1,2,0:T(8,128)(2,1)S(1)}, bf16[2,512,1,128]{3,1,2,0:T(8,128)(2,1)S(1)}, u32[]{:S(2)}, u32[]{:S(2)}) %collective-permute-start) | collective-permute-done | bytes 262176 | tf_op jit(solution)/shard_map/while/body/eval_jaxpr/ppermute | solution.py:13
  180.3 1.6 broadcast_in_dim.75
  184.0 14.9 %collective-permute-done = bf16[2,512,1,128]{3,1,2,0:T(8,128)(2,1)S(1)} collective-permute-done((bf16[2,512,1,128]{3,1,2,0:T(8,128)(2,1)S(1)}, bf16[2,512,1,128]{3,1,2,0:T(8,128)(2,1)S(1)}, u32[]{:S(2)}, u32[]{:S(2)}) %collective-permute-start) | collective-permute-done | bytes 262176 | tf_op jit(solution)/shard_map/while/body/eval_jaxpr/ppermute | solution.py:13
  199.8 1.6 broadcast_in_dim.75
  203.5 14.9 %collective-permute-done = bf16[2,512,1,128]{3,1,2,0:T(8,128)(2,1)S(1)} collective-permute-done((bf16[2,512,1,128]{3,1,2,0:T(8,128)(2,1)S(1)}, bf16[2,512,1,128]{3,1,2,0:T(8,128)(2,1)S(1)}, u32[]{:S(2)}, u32[]{:S(2)}) %collective-permute-start) | collective-permute-done | bytes 262176 | tf_op jit(solution)/shard_map/while/body/eval_jaxpr/ppermute | solution.py:13
  219.3 1.6 broadcast_in_dim.75
  223.0 14.9 %collective-permute-done = bf16[2,512,1,128]{3,1,2,0:T(8,128)(2,1)S(1)} collective-permute-done((bf16[2,512,1,128]{3,1,2,0:T(8,128)(2,1)S(1)}, bf16[2,512,1,128]{3,1,2,0:T(8,128)(2,1)S(1)}, u32[]{:S(2)}, u32[]{:S(2)}) %collective-permute-start) | collective-permute-done | bytes 262176 | tf_op jit(solution)/shard_map/while/body/eval_jaxpr/ppermute | solution.py:13
  242.4 14.9 %collective-permute-done = bf16[2,512,1,128]{3,1,2,0:T(8,128)(2,1)S(1)} collective-permute-done((bf16[2,512,1,128]{3,1,2,0:T(8,128)(2,1)S(1)}, bf16[2,512,1,128]{3,1,2,0:T(8,128)(2,1)S(1)}, u32[]{:S(2)}, u32[]{:S(2)}) %collective-permute-start) | collective-permute-done | bytes 262176 | tf_op jit(solution)/shard_map/while/body/eval_jaxpr/ppermute | solution.py:13
  258.2 1.6 broadcast_in_dim.75
  261.9 14.9 %collective-permute-done = bf16[2,512,1,128]{3,1,2,0:T(8,128)(2,1)S(1)} collective-permute-done((bf16[2,512,1,128]{3,1,2,0:T(8,128)(2,1)S(1)}, bf16[2,512,1,128]{3,1,2,0:T(8,128)(2,1)S(1)}, u32[]{:S(2)}, u32[]{:S(2)}) %collective-permute-start) | collective-permute-done | bytes 262176 | tf_op jit(solution)/shard_map/while/body/eval_jaxpr/ppermute | solution.py:13
  277.7 1.6 broadcast_in_dim.75
  281.4 14.9 %collective-permute-done = bf16[2,512,1,128]{3,1,2,0:T(8,128)(2,1)S(1)} collective-permute-done((bf16[2,512,1,128]{3,1,2,0:T(8,128)(2,1)S(1)}, bf16[2,512,1,128]{3,1,2,0:T(8,128)(2,1)S(1)}, u32[]{:S(2)}, u32[]{:S(2)}) %collective-permute-start) | collective-permute-done | bytes 262176 | tf_op jit(solution)/shard_map/while/body/eval_jaxpr/ppermute | solution.py:13
  297.2 1.6 broadcast_in_dim.75
  300.9 14.9 %collective-permute-done = bf16[2,512,1,128]{3,1,2,0:T(8,128)(2,1)S(1)} collective-permute-done((bf16[2,512,1,128]{3,1,2,0:T(8,128)(2,1)S(1)}, bf16[2,512,1,128]{3,1,2,0:T(8,128)(2,1)S(1)}, u32[]{:S(2)}, u32[]{:S(2)}) %collective-permute-start) | collective-permute-done | bytes 262176 | tf_op jit(solution)/shard_map/while/body/eval_jaxpr/ppermute | solution.py:13
  320.4 14.9 %collective-permute-done = bf16[2,512,1,128]{3,1,2,0:T(8,128)(2,1)S(1)} collective-permute-done((bf16[2,512,1,128]{3,1,2,0:T(8,128)(2,1)S(1)}, bf16[2,512,1,128]{3,1,2,0:T(8,128)(2,1)S(1)}, u32[]{:S(2)}, u32[]{:S(2)}) %collective-permute-start) | collective-permute-done | bytes 262176 | tf_op jit(solution)/shard_map/while/body/eval_jaxpr/ppermute | solution.py:13
  336.2 1.6 broadcast_in_dim.75
  339.9 14.9 %collective-permute-done = bf16[2,512,1,128]{3,1,2,0:T(8,128)(2,1)S(1)} collective-permute-done((bf16[2,512,1,128]{3,1,2,0:T(8,128)(2,1)S(1)}, bf16[2,512,1,128]{3,1,2,0:T(8,128)(2,1)S(1)}, u32[]{:S(2)}, u32[]{:S(2)}) %collective-permute-start) | collective-permute-done | bytes 262176 | tf_op jit(solution)/shard_map/while/body/eval_jaxpr/ppermute | solution.py:13
  355.6 1.6 broadcast_in_dim.75
  359.3 14.9 %collective-permute-done = bf16[2,512,1,128]{3,1,2,0:T(8,128)(2,1)S(1)} collective-permute-done((bf16[2,512,1,128]{3,1,2,0:T(8,128)(2,1)S(1)}, bf16[2,512,1,128]{3,1,2,0:T(8,128)(2,1)S(1)}, u32[]{:S(2)}, u32[]{:S(2)}) %collective-permute-start) | collective-permute-done | bytes 262176 | tf_op jit(solution)/shard_map/while/body/eval_jaxpr/ppermute | solution.py:13
  378.8 14.9 %collective-permute-done = bf16[2,512,1,128]{3,1,2,0:T(8,128)(2,1)S(1)} collective-permute-done((bf16[2,512,1,128]{3,1,2,0:T(8,128)(2,1)S(1)}, bf16[2,512,1,128]{3,1,2,0:T(8,128)(2,1)S(1)}, u32[]{:S(2)}, u32[]{:S(2)}) %collective-permute-start) | collective-permute-done | bytes 262176 | tf_op jit(solution)/shard_map/while/body/eval_jaxpr/ppermute | solution.py:13
  394.6 1.6 broadcast_in_dim.75
  398.3 14.9 %collective-permute-done = bf16[2,512,1,128]{3,1,2,0:T(8,128)(2,1)S(1)} collective-permute-done((bf16[2,512,1,128]{3,1,2,0:T(8,128)(2,1)S(1)}, bf16[2,512,1,128]{3,1,2,0:T(8,128)(2,1)S(1)}, u32[]{:S(2)}, u32[]{:S(2)}) %collective-permute-start) | collective-permute-done | bytes 262176 | tf_op jit(solution)/shard_map/while/body/eval_jaxpr/ppermute | solution.py:13
  414.1 1.6 broadcast_in_dim.75
  417.8 14.9 %collective-permute-done = bf16[2,512,1,128]{3,1,2,0:T(8,128)(2,1)S(1)} collective-permute-done((bf16[2,512,1,128]{3,1,2,0:T(8,128)(2,1)S(1)}, bf16[2,512,1,128]{3,1,2,0:T(8,128)(2,1)S(1)}, u32[]{:S(2)}, u32[]{:S(2)}) %collective-permute-start) | collective-permute-done | bytes 262176 | tf_op jit(solution)/shard_map/while/body/eval_jaxpr/ppermute | solution.py:13
  433.6 1.6 broadcast_in_dim.75
  437.3 14.9 %collective-permute-done = bf16[2,512,1,128]{3,1,2,0:T(8,128)(2,1)S(1)} collective-permute-done((bf16[2,512,1,128]{3,1,2,0:T(8,128)(2,1)S(1)}, bf16[2,512,1,128]{3,1,2,0:T(8,128)(2,1)S(1)}, u32[]{:S(2)}, u32[]{:S(2)}) %collective-permute-start) | collective-permute-done | bytes 262176 | tf_op jit(solution)/shard_map/while/body/eval_jaxpr/ppermute | solution.py:13
  456.8 14.9 %collective-permute-done = bf16[2,512,1,128]{3,1,2,0:T(8,128)(2,1)S(1)} collective-permute-done((bf16[2,512,1,128]{3,1,2,0:T(8,128)(2,1)S(1)}, bf16[2,512,1,128]{3,1,2,0:T(8,128)(2,1)S(1)}, u32[]{:S(2)}, u32[]{:S(2)}) %collective-permute-start) | collective-permute-done | bytes 262176 | tf_op jit(solution)/shard_map/while/body/eval_jaxpr/ppermute | solution.py:13
  472.5 1.6 broadcast_in_dim.75
  476.2 14.9 %collective-permute-done = bf16[2,512,1,128]{3,1,2,0:T(8,128)(2,1)S(1)} collective-permute-done((bf16[2,512,1,128]{3,1,2,0:T(8,128)(2,1)S(1)}, bf16[2,512,1,128]{3,1,2,0:T(8,128)(2,1)S(1)}, u32[]{:S(2)}, u32[]{:S(2)}) %collective-permute-start) | collective-permute-done | bytes 262176 | tf_op jit(solution)/shard_map/while/body/eval_jaxpr/ppermute | solution.py:13
  492.0 1.6 broadcast_in_dim.75
  495.7 14.9 %collective-permute-done = bf16[2,512,1,128]{3,1,2,0:T(8,128)(2,1)S(1)} collective-permute-done((bf16[2,512,1,128]{3,1,2,0:T(8,128)(2,1)S(1)}, bf16[2,512,1,128]{3,1,2,0:T(8,128)(2,1)S(1)}, u32[]{:S(2)}, u32[]{:S(2)}) %collective-permute-start) | collective-permute-done | bytes 262176 | tf_op jit(solution)/shard_map/while/body/eval_jaxpr/ppermute | solution.py:13
  511.5 1.6 broadcast_in_dim.75
  515.2 14.9 %collective-permute-done = bf16[2,512,1,128]{3,1,2,0:T(8,128)(2,1)S(1)} collective-permute-done((bf16[2,512,1,128]{3,1,2,0:T(8,128)(2,1)S(1)}, bf16[2,512,1,128]{3,1,2,0:T(8,128)(2,1)S(1)}, u32[]{:S(2)}, u32[]{:S(2)}) %collective-permute-start) | collective-permute-done | bytes 262176 | tf_op jit(solution)/shard_map/while/body/eval_jaxpr/ppermute | solution.py:13
  534.7 14.9 %collective-permute-done = bf16[2,512,1,128]{3,1,2,0:T(8,128)(2,1)S(1)} collective-permute-done((bf16[2,512,1,128]{3,1,2,0:T(8,128)(2,1)S(1)}, bf16[2,512,1,128]{3,1,2,0:T(8,128)(2,1)S(1)}, u32[]{:S(2)}, u32[]{:S(2)}) %collective-permute-start) | collective-permute-done | bytes 262176 | tf_op jit(solution)/shard_map/while/body/eval_jaxpr/ppermute | solution.py:13
  554.2 14.9 %collective-permute-done = bf16[2,512,1,128]{3,1,2,0:T(8,128)(2,1)S(1)} collective-permute-done((bf16[2,512,1,128]{3,1,2,0:T(8,128)(2,1)S(1)}, bf16[2,512,1,128]{3,1,2,0:T(8,128)(2,1)S(1)}, u32[]{:S(2)}, u32[]{:S(2)}) %collective-permute-start) | collective-permute-done | bytes 262176 | tf_op jit(solution)/shard_map/while/body/eval_jaxpr/ppermute | solution.py:13
  573.6 14.9 %collective-permute-done = bf16[2,512,1,128]{3,1,2,0:T(8,128)(2,1)S(1)} collective-permute-done((bf16[2,512,1,128]{3,1,2,0:T(8,128)(2,1)S(1)}, bf16[2,512,1,128]{3,1,2,0:T(8,128)(2,1)S(1)}, u32[]{:S(2)}, u32[]{:S(2)}) %collective-permute-start) | collective-permute-done | bytes 262176 | tf_op jit(solution)/shard_map/while/body/eval_jaxpr/ppermute | solution.py:13
  593.1 14.9 %collective-permute-done = bf16[2,512,1,128]{3,1,2,0:T(8,128)(2,1)S(1)} collective-permute-done((bf16[2,512,1,128]{3,1,2,0:T(8,128)(2,1)S(1)}, bf16[2,512,1,128]{3,1,2,0:T(8,128)(2,1)S(1)}, u32[]{:S(2)}, u32[]{:S(2)}) %collective-permute-start) | collective-permute-done | bytes 262176 | tf_op jit(solution)/shard_map/while/body/eval_jaxpr/ppermute | solution.py:13
  612.6 14.9 %collective-permute-done = bf16[2,512,1,128]{3,1,2,0:T(8,128)(2,1)S(1)} collective-permute-done((bf16[2,512,1,128]{3,1,2,0:T(8,128)(2,1)S(1)}, bf16[2,512,1,128]{3,1,2,0:T(8,128)(2,1)S(1)}, u32[]{:S(2)}, u32[]{:S(2)}) %collective-permute-start) | collective-permute-done | bytes 262176 | tf_op jit(solution)/shard_map/while/body/eval_jaxpr/ppermute | solution.py:13
  629.1 2.0 fusion.32
  631.2 7.6 %collective-permute-done.2 = bf16[2,512,1,128]{3,1,2,0:T(8,128)(2,1)S(1)} collective-permute-done((bf16[2,512,1,128]{3,1,2,0:T(8,128)(2,1)S(1)}, bf16[2,512,1,128]{3,1,2,0:T(8,128)(2,1)S(1)}, u32[]{:S(2)}, u32[]{:S(2)}) %collective-permute-start.2) | collective-permute-done | bytes 262176 | tf_op jit(solution)/shard_map/ppermute | solution.py:13
  639.2 1.8 add_bitcast_fusion
  641.0 112.0 %reduce-scatter.2.cloned.1.call-done = f32[128,512]{0,1:T(8,128)} async-done(((f32[1024,512]{0,1:T(8,128)}), f32[128,512]{0,1:T(8,128)}) %reduce-scatter.2.cloned.1.call-update) | async-done | bytes 262160 | tf_op jit(solution)/shard_map/reduce_scatter | solution.py:125
  753.0 1.6 convert_bitcast_fusion
  (459 shorter events, 114.7 us)
Async XLA Ops:
  8.7 32.9 %all-to-all-start = ((bf16[8,512,128]{1,2,0:T(8,128)(2,1)}), bf16[8,512,128]{1,2,0:T(8,128)(2,1)S(1)}, u32[]{:S(2)}, u32[]{:S(2)}) async-start(bf16[8,512,128]{1,2,0:T(8,128)(2,1)} %stack.68), calls=%async_computation | async-start | bytes 2097152 | tf_op jit(solution)/shard_map/all_to_all | solution.py:66
  19.7 733.4 %reduce-scatter.2.cloned.1.call-start = ((), (), s32[]{:S(2)}) async-start(), calls=%async_computation.2 | async-start | bytes 2359296 | tf_op jit(solution)/shard_map/reduce_scatter | solution.py:125
  46.2 11.5 %collective-permute-start.1 = (f32[2,512,1,128]{3,1,2,0:T(8,128)S(1)}, f32[2,512,1,128]{3,1,2,0:T(8,128)S(1)}, u32[]{:S(2)}, u32[]{:S(2)}) collective-permute-start(f32[2,512,1,128]{3,1,2,0:T(8,128)S(1)} %convert_add_fusion.3), channel_id=1, source_target_pairs={{0,8},{8,16},{16,24},{24,32},{32,40},{40,48},{48,56},{56,64},{64,7... | collective-permute-start | bytes 1572872 | tf_op jit(solution)/shard_map/while/body/eval_jaxpr/ppermute | solution.py:13
  46.3 11.4 %collective-permute-start = (bf16[2,512,1,128]{3,1,2,0:T(8,128)(2,1)S(1)}, bf16[2,512,1,128]{3,1,2,0:T(8,128)(2,1)S(1)}, u32[]{:S(2)}, u32[]{:S(2)}) collective-permute-start(bf16[2,512,1,128]{3,1,2,0:T(8,128)(2,1)S(1)} %copy.51), channel_id=1, source_target_pairs={{0,8},{8,16},{16,24},{24,32},{32,40},{40,48},{48,56},{56,64},{64,7... | collective-permute-start | bytes 786440 | tf_op jit(solution)/shard_map/while/body/eval_jaxpr/ppermute | solution.py:13
  61.8 11.5 %collective-permute-start.1 = (f32[2,512,1,128]{3,1,2,0:T(8,128)S(1)}, f32[2,512,1,128]{3,1,2,0:T(8,128)S(1)}, u32[]{:S(2)}, u32[]{:S(2)}) collective-permute-start(f32[2,512,1,128]{3,1,2,0:T(8,128)S(1)} %convert_add_fusion.3), channel_id=1, source_target_pairs={{0,8},{8,16},{16,24},{24,32},{32,40},{40,48},{48,56},{56,64},{64,7... | collective-permute-start | bytes 1572872 | tf_op jit(solution)/shard_map/while/body/eval_jaxpr/ppermute | solution.py:13
  61.9 11.4 %collective-permute-start = (bf16[2,512,1,128]{3,1,2,0:T(8,128)(2,1)S(1)}, bf16[2,512,1,128]{3,1,2,0:T(8,128)(2,1)S(1)}, u32[]{:S(2)}, u32[]{:S(2)}) collective-permute-start(bf16[2,512,1,128]{3,1,2,0:T(8,128)(2,1)S(1)} %copy.51), channel_id=1, source_target_pairs={{0,8},{8,16},{16,24},{24,32},{32,40},{40,48},{48,56},{56,64},{64,7... | collective-permute-start | bytes 786440 | tf_op jit(solution)/shard_map/while/body/eval_jaxpr/ppermute | solution.py:13
  77.4 11.5 %collective-permute-start.1 = (f32[2,512,1,128]{3,1,2,0:T(8,128)S(1)}, f32[2,512,1,128]{3,1,2,0:T(8,128)S(1)}, u32[]{:S(2)}, u32[]{:S(2)}) collective-permute-start(f32[2,512,1,128]{3,1,2,0:T(8,128)S(1)} %convert_add_fusion.3), channel_id=1, source_target_pairs={{0,8},{8,16},{16,24},{24,32},{32,40},{40,48},{48,56},{56,64},{64,7... | collective-permute-start | bytes 1572872 | tf_op jit(solution)/shard_map/while/body/eval_jaxpr/ppermute | solution.py:13
  77.5 11.4 %collective-permute-start = (bf16[2,512,1,128]{3,1,2,0:T(8,128)(2,1)S(1)}, bf16[2,512,1,128]{3,1,2,0:T(8,128)(2,1)S(1)}, u32[]{:S(2)}, u32[]{:S(2)}) collective-permute-start(bf16[2,512,1,128]{3,1,2,0:T(8,128)(2,1)S(1)} %copy.51), channel_id=1, source_target_pairs={{0,8},{8,16},{16,24},{24,32},{32,40},{40,48},{48,56},{56,64},{64,7... | collective-permute-start | bytes 786440 | tf_op jit(solution)/shard_map/while/body/eval_jaxpr/ppermute | solution.py:13
  93.0 11.5 %collective-permute-start.1 = (f32[2,512,1,128]{3,1,2,0:T(8,128)S(1)}, f32[2,512,1,128]{3,1,2,0:T(8,128)S(1)}, u32[]{:S(2)}, u32[]{:S(2)}) collective-permute-start(f32[2,512,1,128]{3,1,2,0:T(8,128)S(1)} %convert_add_fusion.3), channel_id=1, source_target_pairs={{0,8},{8,16},{16,24},{24,32},{32,40},{40,48},{48,56},{56,64},{64,7... | collective-permute-start | bytes 1572872 | tf_op jit(solution)/shard_map/while/body/eval_jaxpr/ppermute | solution.py:13
  93.1 11.4 %collective-permute-start = (bf16[2,512,1,128]{3,1,2,0:T(8,128)(2,1)S(1)}, bf16[2,512,1,128]{3,1,2,0:T(8,128)(2,1)S(1)}, u32[]{:S(2)}, u32[]{:S(2)}) collective-permute-start(bf16[2,512,1,128]{3,1,2,0:T(8,128)(2,1)S(1)} %copy.51), channel_id=1, source_target_pairs={{0,8},{8,16},{16,24},{24,32},{32,40},{40,48},{48,56},{56,64},{64,7... | collective-permute-start | bytes 786440 | tf_op jit(solution)/shard_map/while/body/eval_jaxpr/ppermute | solution.py:13
  108.5 12.4 %collective-permute-start.1 = (f32[2,512,1,128]{3,1,2,0:T(8,128)S(1)}, f32[2,512,1,128]{3,1,2,0:T(8,128)S(1)}, u32[]{:S(2)}, u32[]{:S(2)}) collective-permute-start(f32[2,512,1,128]{3,1,2,0:T(8,128)S(1)} %convert_add_fusion.3), channel_id=1, source_target_pairs={{0,8},{8,16},{16,24},{24,32},{32,40},{40,48},{48,56},{56,64},{64,7... | collective-permute-start | bytes 1572872 | tf_op jit(solution)/shard_map/while/body/eval_jaxpr/ppermute | solution.py:13
  108.6 12.3 %collective-permute-start = (bf16[2,512,1,128]{3,1,2,0:T(8,128)(2,1)S(1)}, bf16[2,512,1,128]{3,1,2,0:T(8,128)(2,1)S(1)}, u32[]{:S(2)}, u32[]{:S(2)}) collective-permute-start(bf16[2,512,1,128]{3,1,2,0:T(8,128)(2,1)S(1)} %copy.51), channel_id=1, source_target_pairs={{0,8},{8,16},{16,24},{24,32},{32,40},{40,48},{48,56},{56,64},{64,7... | collective-permute-start | bytes 786440 | tf_op jit(solution)/shard_map/while/body/eval_jaxpr/ppermute | solution.py:13
  125.0 15.4 %collective-permute-start.1 = (f32[2,512,1,128]{3,1,2,0:T(8,128)S(1)}, f32[2,512,1,128]{3,1,2,0:T(8,128)S(1)}, u32[]{:S(2)}, u32[]{:S(2)}) collective-permute-start(f32[2,512,1,128]{3,1,2,0:T(8,128)S(1)} %convert_add_fusion.3), channel_id=1, source_target_pairs={{0,8},{8,16},{16,24},{24,32},{32,40},{40,48},{48,56},{56,64},{64,7... | collective-permute-start | bytes 1572872 | tf_op jit(solution)/shard_map/while/body/eval_jaxpr/ppermute | solution.py:13
  125.1 15.3 %collective-permute-start = (bf16[2,512,1,128]{3,1,2,0:T(8,128)(2,1)S(1)}, bf16[2,512,1,128]{3,1,2,0:T(8,128)(2,1)S(1)}, u32[]{:S(2)}, u32[]{:S(2)}) collective-permute-start(bf16[2,512,1,128]{3,1,2,0:T(8,128)(2,1)S(1)} %copy.51), channel_id=1, source_target_pairs={{0,8},{8,16},{16,24},{24,32},{32,40},{40,48},{48,56},{56,64},{64,7... | collective-permute-start | bytes 786440 | tf_op jit(solution)/shard_map/while/body/eval_jaxpr/ppermute | solution.py:13
  144.5 15.4 %collective-permute-start.1 = (f32[2,512,1,128]{3,1,2,0:T(8,128)S(1)}, f32[2,512,1,128]{3,1,2,0:T(8,128)S(1)}, u32[]{:S(2)}, u32[]{:S(2)}) collective-permute-start(f32[2,512,1,128]{3,1,2,0:T(8,128)S(1)} %convert_add_fusion.3), channel_id=1, source_target_pairs={{0,8},{8,16},{16,24},{24,32},{32,40},{40,48},{48,56},{56,64},{64,7... | collective-permute-start | bytes 1572872 | tf_op jit(solution)/shard_map/while/body/eval_jaxpr/ppermute | solution.py:13
  144.6 15.3 %collective-permute-start = (bf16[2,512,1,128]{3,1,2,0:T(8,128)(2,1)S(1)}, bf16[2,512,1,128]{3,1,2,0:T(8,128)(2,1)S(1)}, u32[]{:S(2)}, u32[]{:S(2)}) collective-permute-start(bf16[2,512,1,128]{3,1,2,0:T(8,128)(2,1)S(1)} %copy.51), channel_id=1, source_target_pairs={{0,8},{8,16},{16,24},{24,32},{32,40},{40,48},{48,56},{56,64},{64,7... | collective-permute-start | bytes 786440 | tf_op jit(solution)/shard_map/while/body/eval_jaxpr/ppermute | solution.py:13
  164.0 15.4 %collective-permute-start.1 = (f32[2,512,1,128]{3,1,2,0:T(8,128)S(1)}, f32[2,512,1,128]{3,1,2,0:T(8,128)S(1)}, u32[]{:S(2)}, u32[]{:S(2)}) collective-permute-start(f32[2,512,1,128]{3,1,2,0:T(8,128)S(1)} %convert_add_fusion.3), channel_id=1, source_target_pairs={{0,8},{8,16},{16,24},{24,32},{32,40},{40,48},{48,56},{56,64},{64,7... | collective-permute-start | bytes 1572872 | tf_op jit(solution)/shard_map/while/body/eval_jaxpr/ppermute | solution.py:13
  164.1 15.3 %collective-permute-start = (bf16[2,512,1,128]{3,1,2,0:T(8,128)(2,1)S(1)}, bf16[2,512,1,128]{3,1,2,0:T(8,128)(2,1)S(1)}, u32[]{:S(2)}, u32[]{:S(2)}) collective-permute-start(bf16[2,512,1,128]{3,1,2,0:T(8,128)(2,1)S(1)} %copy.51), channel_id=1, source_target_pairs={{0,8},{8,16},{16,24},{24,32},{32,40},{40,48},{48,56},{56,64},{64,7... | collective-permute-start | bytes 786440 | tf_op jit(solution)/shard_map/while/body/eval_jaxpr/ppermute | solution.py:13
  183.5 15.4 %collective-permute-start.1 = (f32[2,512,1,128]{3,1,2,0:T(8,128)S(1)}, f32[2,512,1,128]{3,1,2,0:T(8,128)S(1)}, u32[]{:S(2)}, u32[]{:S(2)}) collective-permute-start(f32[2,512,1,128]{3,1,2,0:T(8,128)S(1)} %convert_add_fusion.3), channel_id=1, source_target_pairs={{0,8},{8,16},{16,24},{24,32},{32,40},{40,48},{48,56},{56,64},{64,7... | collective-permute-start | bytes 1572872 | tf_op jit(solution)/shard_map/while/body/eval_jaxpr/ppermute | solution.py:13
  183.6 15.3 %collective-permute-start = (bf16[2,512,1,128]{3,1,2,0:T(8,128)(2,1)S(1)}, bf16[2,512,1,128]{3,1,2,0:T(8,128)(2,1)S(1)}, u32[]{:S(2)}, u32[]{:S(2)}) collective-permute-start(bf16[2,512,1,128]{3,1,2,0:T(8,128)(2,1)S(1)} %copy.51), channel_id=1, source_target_pairs={{0,8},{8,16},{16,24},{24,32},{32,40},{40,48},{48,56},{56,64},{64,7... | collective-permute-start | bytes 786440 | tf_op jit(solution)/shard_map/while/body/eval_jaxpr/ppermute | solution.py:13
  203.0 15.4 %collective-permute-start.1 = (f32[2,512,1,128]{3,1,2,0:T(8,128)S(1)}, f32[2,512,1,128]{3,1,2,0:T(8,128)S(1)}, u32[]{:S(2)}, u32[]{:S(2)}) collective-permute-start(f32[2,512,1,128]{3,1,2,0:T(8,128)S(1)} %convert_add_fusion.3), channel_id=1, source_target_pairs={{0,8},{8,16},{16,24},{24,32},{32,40},{40,48},{48,56},{56,64},{64,7... | collective-permute-start | bytes 1572872 | tf_op jit(solution)/shard_map/while/body/eval_jaxpr/ppermute | solution.py:13
  203.0 15.3 %collective-permute-start = (bf16[2,512,1,128]{3,1,2,0:T(8,128)(2,1)S(1)}, bf16[2,512,1,128]{3,1,2,0:T(8,128)(2,1)S(1)}, u32[]{:S(2)}, u32[]{:S(2)}) collective-permute-start(bf16[2,512,1,128]{3,1,2,0:T(8,128)(2,1)S(1)} %copy.51), channel_id=1, source_target_pairs={{0,8},{8,16},{16,24},{24,32},{32,40},{40,48},{48,56},{56,64},{64,7... | collective-permute-start | bytes 786440 | tf_op jit(solution)/shard_map/while/body/eval_jaxpr/ppermute | solution.py:13
  222.4 15.4 %collective-permute-start.1 = (f32[2,512,1,128]{3,1,2,0:T(8,128)S(1)}, f32[2,512,1,128]{3,1,2,0:T(8,128)S(1)}, u32[]{:S(2)}, u32[]{:S(2)}) collective-permute-start(f32[2,512,1,128]{3,1,2,0:T(8,128)S(1)} %convert_add_fusion.3), channel_id=1, source_target_pairs={{0,8},{8,16},{16,24},{24,32},{32,40},{40,48},{48,56},{56,64},{64,7... | collective-permute-start | bytes 1572872 | tf_op jit(solution)/shard_map/while/body/eval_jaxpr/ppermute | solution.py:13
  222.5 15.3 %collective-permute-start = (bf16[2,512,1,128]{3,1,2,0:T(8,128)(2,1)S(1)}, bf16[2,512,1,128]{3,1,2,0:T(8,128)(2,1)S(1)}, u32[]{:S(2)}, u32[]{:S(2)}) collective-permute-start(bf16[2,512,1,128]{3,1,2,0:T(8,128)(2,1)S(1)} %copy.51), channel_id=1, source_target_pairs={{0,8},{8,16},{16,24},{24,32},{32,40},{40,48},{48,56},{56,64},{64,7... | collective-permute-start | bytes 786440 | tf_op jit(solution)/shard_map/while/body/eval_jaxpr/ppermute | solution.py:13
  241.9 15.4 %collective-permute-start.1 = (f32[2,512,1,128]{3,1,2,0:T(8,128)S(1)}, f32[2,512,1,128]{3,1,2,0:T(8,128)S(1)}, u32[]{:S(2)}, u32[]{:S(2)}) collective-permute-start(f32[2,512,1,128]{3,1,2,0:T(8,128)S(1)} %convert_add_fusion.3), channel_id=1, source_target_pairs={{0,8},{8,16},{16,24},{24,32},{32,40},{40,48},{48,56},{56,64},{64,7... | collective-permute-start | bytes 1572872 | tf_op jit(solution)/shard_map/while/body/eval_jaxpr/ppermute | solution.py:13
  242.0 15.3 %collective-permute-start = (bf16[2,512,1,128]{3,1,2,0:T(8,128)(2,1)S(1)}, bf16[2,512,1,128]{3,1,2,0:T(8,128)(2,1)S(1)}, u32[]{:S(2)}, u32[]{:S(2)}) collective-permute-start(bf16[2,512,1,128]{3,1,2,0:T(8,128)(2,1)S(1)} %copy.51), channel_id=1, source_target_pairs={{0,8},{8,16},{16,24},{24,32},{32,40},{40,48},{48,56},{56,64},{64,7... | collective-permute-start | bytes 786440 | tf_op jit(solution)/shard_map/while/body/eval_jaxpr/ppermute | solution.py:13
  261.4 15.4 %collective-permute-start.1 = (f32[2,512,1,128]{3,1,2,0:T(8,128)S(1)}, f32[2,512,1,128]{3,1,2,0:T(8,128)S(1)}, u32[]{:S(2)}, u32[]{:S(2)}) collective-permute-start(f32[2,512,1,128]{3,1,2,0:T(8,128)S(1)} %convert_add_fusion.3), channel_id=1, source_target_pairs={{0,8},{8,16},{16,24},{24,32},{32,40},{40,48},{48,56},{56,64},{64,7... | collective-permute-start | bytes 1572872 | tf_op jit(solution)/shard_map/while/body/eval_jaxpr/ppermute | solution.py:13
  261.5 15.3 %collective-permute-start = (bf16[2,512,1,128]{3,1,2,0:T(8,128)(2,1)S(1)}, bf16[2,512,1,128]{3,1,2,0:T(8,128)(2,1)S(1)}, u32[]{:S(2)}, u32[]{:S(2)}) collective-permute-start(bf16[2,512,1,128]{3,1,2,0:T(8,128)(2,1)S(1)} %copy.51), channel_id=1, source_target_pairs={{0,8},{8,16},{16,24},{24,32},{32,40},{40,48},{48,56},{56,64},{64,7... | collective-permute-start | bytes 786440 | tf_op jit(solution)/shard_map/while/body/eval_jaxpr/ppermute | solution.py:13
  280.9 15.4 %collective-permute-start.1 = (f32[2,512,1,128]{3,1,2,0:T(8,128)S(1)}, f32[2,512,1,128]{3,1,2,0:T(8,128)S(1)}, u32[]{:S(2)}, u32[]{:S(2)}) collective-permute-start(f32[2,512,1,128]{3,1,2,0:T(8,128)S(1)} %convert_add_fusion.3), channel_id=1, source_target_pairs={{0,8},{8,16},{16,24},{24,32},{32,40},{40,48},{48,56},{56,64},{64,7... | collective-permute-start | bytes 1572872 | tf_op jit(solution)/shard_map/while/body/eval_jaxpr/ppermute | solution.py:13
  281.0 15.3 %collective-permute-start = (bf16[2,512,1,128]{3,1,2,0:T(8,128)(2,1)S(1)}, bf16[2,512,1,128]{3,1,2,0:T(8,128)(2,1)S(1)}, u32[]{:S(2)}, u32[]{:S(2)}) collective-permute-start(bf16[2,512,1,128]{3,1,2,0:T(8,128)(2,1)S(1)} %copy.51), channel_id=1, source_target_pairs={{0,8},{8,16},{16,24},{24,32},{32,40},{40,48},{48,56},{56,64},{64,7... | collective-permute-start | bytes 786440 | tf_op jit(solution)/shard_map/while/body/eval_jaxpr/ppermute | solution.py:13
  300.4 15.4 %collective-permute-start.1 = (f32[2,512,1,128]{3,1,2,0:T(8,128)S(1)}, f32[2,512,1,128]{3,1,2,0:T(8,128)S(1)}, u32[]{:S(2)}, u32[]{:S(2)}) collective-permute-start(f32[2,512,1,128]{3,1,2,0:T(8,128)S(1)} %convert_add_fusion.3), channel_id=1, source_target_pairs={{0,8},{8,16},{16,24},{24,32},{32,40},{40,48},{48,56},{56,64},{64,7... | collective-permute-start | bytes 1572872 | tf_op jit(solution)/shard_map/while/body/eval_jaxpr/ppermute | solution.py:13
  300.5 15.3 %collective-permute-start = (bf16[2,512,1,128]{3,1,2,0:T(8,128)(2,1)S(1)}, bf16[2,512,1,128]{3,1,2,0:T(8,128)(2,1)S(1)}, u32[]{:S(2)}, u32[]{:S(2)}) collective-permute-start(bf16[2,512,1,128]{3,1,2,0:T(8,128)(2,1)S(1)} %copy.51), channel_id=1, source_target_pairs={{0,8},{8,16},{16,24},{24,32},{32,40},{40,48},{48,56},{56,64},{64,7... | collective-permute-start | bytes 786440 | tf_op jit(solution)/shard_map/while/body/eval_jaxpr/ppermute | solution.py:13
  319.9 15.4 %collective-permute-start.1 = (f32[2,512,1,128]{3,1,2,0:T(8,128)S(1)}, f32[2,512,1,128]{3,1,2,0:T(8,128)S(1)}, u32[]{:S(2)}, u32[]{:S(2)}) collective-permute-start(f32[2,512,1,128]{3,1,2,0:T(8,128)S(1)} %convert_add_fusion.3), channel_id=1, source_target_pairs={{0,8},{8,16},{16,24},{24,32},{32,40},{40,48},{48,56},{56,64},{64,7... | collective-permute-start | bytes 1572872 | tf_op jit(solution)/shard_map/while/body/eval_jaxpr/ppermute | solution.py:13
  319.9 15.3 %collective-permute-start = (bf16[2,512,1,128]{3,1,2,0:T(8,128)(2,1)S(1)}, bf16[2,512,1,128]{3,1,2,0:T(8,128)(2,1)S(1)}, u32[]{:S(2)}, u32[]{:S(2)}) collective-permute-start(bf16[2,512,1,128]{3,1,2,0:T(8,128)(2,1)S(1)} %copy.51), channel_id=1, source_target_pairs={{0,8},{8,16},{16,24},{24,32},{32,40},{40,48},{48,56},{56,64},{64,7... | collective-permute-start | bytes 786440 | tf_op jit(solution)/shard_map/while/body/eval_jaxpr/ppermute | solution.py:13
  339.3 15.4 %collective-permute-start.1 = (f32[2,512,1,128]{3,1,2,0:T(8,128)S(1)}, f32[2,512,1,128]{3,1,2,0:T(8,128)S(1)}, u32[]{:S(2)}, u32[]{:S(2)}) collective-permute-start(f32[2,512,1,128]{3,1,2,0:T(8,128)S(1)} %convert_add_fusion.3), channel_id=1, source_target_pairs={{0,8},{8,16},{16,24},{24,32},{32,40},{40,48},{48,56},{56,64},{64,7... | collective-permute-start | bytes 1572872 | tf_op jit(solution)/shard_map/while/body/eval_jaxpr/ppermute | solution.py:13
  339.4 15.3 %collective-permute-start = (bf16[2,512,1,128]{3,1,2,0:T(8,128)(2,1)S(1)}, bf16[2,512,1,128]{3,1,2,0:T(8,128)(2,1)S(1)}, u32[]{:S(2)}, u32[]{:S(2)}) collective-permute-start(bf16[2,512,1,128]{3,1,2,0:T(8,128)(2,1)S(1)} %copy.51), channel_id=1, source_target_pairs={{0,8},{8,16},{16,24},{24,32},{32,40},{40,48},{48,56},{56,64},{64,7... | collective-permute-start | bytes 786440 | tf_op jit(solution)/shard_map/while/body/eval_jaxpr/ppermute | solution.py:13
  358.8 15.4 %collective-permute-start.1 = (f32[2,512,1,128]{3,1,2,0:T(8,128)S(1)}, f32[2,512,1,128]{3,1,2,0:T(8,128)S(1)}, u32[]{:S(2)}, u32[]{:S(2)}) collective-permute-start(f32[2,512,1,128]{3,1,2,0:T(8,128)S(1)} %convert_add_fusion.3), channel_id=1, source_target_pairs={{0,8},{8,16},{16,24},{24,32},{32,40},{40,48},{48,56},{56,64},{64,7... | collective-permute-start | bytes 1572872 | tf_op jit(solution)/shard_map/while/body/eval_jaxpr/ppermute | solution.py:13
  358.9 15.3 %collective-permute-start = (bf16[2,512,1,128]{3,1,2,0:T(8,128)(2,1)S(1)}, bf16[2,512,1,128]{3,1,2,0:T(8,128)(2,1)S(1)}, u32[]{:S(2)}, u32[]{:S(2)}) collective-permute-start(bf16[2,512,1,128]{3,1,2,0:T(8,128)(2,1)S(1)} %copy.51), channel_id=1, source_target_pairs={{0,8},{8,16},{16,24},{24,32},{32,40},{40,48},{48,56},{56,64},{64,7... | collective-permute-start | bytes 786440 | tf_op jit(solution)/shard_map/while/body/eval_jaxpr/ppermute | solution.py:13
  378.3 15.4 %collective-permute-start.1 = (f32[2,512,1,128]{3,1,2,0:T(8,128)S(1)}, f32[2,512,1,128]{3,1,2,0:T(8,128)S(1)}, u32[]{:S(2)}, u32[]{:S(2)}) collective-permute-start(f32[2,512,1,128]{3,1,2,0:T(8,128)S(1)} %convert_add_fusion.3), channel_id=1, source_target_pairs={{0,8},{8,16},{16,24},{24,32},{32,40},{40,48},{48,56},{56,64},{64,7... | collective-permute-start | bytes 1572872 | tf_op jit(solution)/shard_map/while/body/eval_jaxpr/ppermute | solution.py:13
  378.4 15.3 %collective-permute-start = (bf16[2,512,1,128]{3,1,2,0:T(8,128)(2,1)S(1)}, bf16[2,512,1,128]{3,1,2,0:T(8,128)(2,1)S(1)}, u32[]{:S(2)}, u32[]{:S(2)}) collective-permute-start(bf16[2,512,1,128]{3,1,2,0:T(8,128)(2,1)S(1)} %copy.51), channel_id=1, source_target_pairs={{0,8},{8,16},{16,24},{24,32},{32,40},{40,48},{48,56},{56,64},{64,7... | collective-permute-start | bytes 786440 | tf_op jit(solution)/shard_map/while/body/eval_jaxpr/ppermute | solution.py:13
  397.8 15.4 %collective-permute-start.1 = (f32[2,512,1,128]{3,1,2,0:T(8,128)S(1)}, f32[2,512,1,128]{3,1,2,0:T(8,128)S(1)}, u32[]{:S(2)}, u32[]{:S(2)}) collective-permute-start(f32[2,512,1,128]{3,1,2,0:T(8,128)S(1)} %convert_add_fusion.3), channel_id=1, source_target_pairs={{0,8},{8,16},{16,24},{24,32},{32,40},{40,48},{48,56},{56,64},{64,7... | collective-permute-start | bytes 1572872 | tf_op jit(solution)/shard_map/while/body/eval_jaxpr/ppermute | solution.py:13
  397.9 15.3 %collective-permute-start = (bf16[2,512,1,128]{3,1,2,0:T(8,128)(2,1)S(1)}, bf16[2,512,1,128]{3,1,2,0:T(8,128)(2,1)S(1)}, u32[]{:S(2)}, u32[]{:S(2)}) collective-permute-start(bf16[2,512,1,128]{3,1,2,0:T(8,128)(2,1)S(1)} %copy.51), channel_id=1, source_target_pairs={{0,8},{8,16},{16,24},{24,32},{32,40},{40,48},{48,56},{56,64},{64,7... | collective-permute-start | bytes 786440 | tf_op jit(solution)/shard_map/while/body/eval_jaxpr/ppermute | solution.py:13
  417.3 15.4 %collective-permute-start.1 = (f32[2,512,1,128]{3,1,2,0:T(8,128)S(1)}, f32[2,512,1,128]{3,1,2,0:T(8,128)S(1)}, u32[]{:S(2)}, u32[]{:S(2)}) collective-permute-start(f32[2,512,1,128]{3,1,2,0:T(8,128)S(1)} %convert_add_fusion.3), channel_id=1, source_target_pairs={{0,8},{8,16},{16,24},{24,32},{32,40},{40,48},{48,56},{56,64},{64,7... | collective-permute-start | bytes 1572872 | tf_op jit(solution)/shard_map/while/body/eval_jaxpr/ppermute | solution.py:13
  417.4 15.3 %collective-permute-start = (bf16[2,512,1,128]{3,1,2,0:T(8,128)(2,1)S(1)}, bf16[2,512,1,128]{3,1,2,0:T(8,128)(2,1)S(1)}, u32[]{:S(2)}, u32[]{:S(2)}) collective-permute-start(bf16[2,512,1,128]{3,1,2,0:T(8,128)(2,1)S(1)} %copy.51), channel_id=1, source_target_pairs={{0,8},{8,16},{16,24},{24,32},{32,40},{40,48},{48,56},{56,64},{64,7... | collective-permute-start | bytes 786440 | tf_op jit(solution)/shard_map/while/body/eval_jaxpr/ppermute | solution.py:13
  436.7 15.4 %collective-permute-start.1 = (f32[2,512,1,128]{3,1,2,0:T(8,128)S(1)}, f32[2,512,1,128]{3,1,2,0:T(8,128)S(1)}, u32[]{:S(2)}, u32[]{:S(2)}) collective-permute-start(f32[2,512,1,128]{3,1,2,0:T(8,128)S(1)} %convert_add_fusion.3), channel_id=1, source_target_pairs={{0,8},{8,16},{16,24},{24,32},{32,40},{40,48},{48,56},{56,64},{64,7... | collective-permute-start | bytes 1572872 | tf_op jit(solution)/shard_map/while/body/eval_jaxpr/ppermute | solution.py:13
  436.8 15.3 %collective-permute-start = (bf16[2,512,1,128]{3,1,2,0:T(8,128)(2,1)S(1)}, bf16[2,512,1,128]{3,1,2,0:T(8,128)(2,1)S(1)}, u32[]{:S(2)}, u32[]{:S(2)}) collective-permute-start(bf16[2,512,1,128]{3,1,2,0:T(8,128)(2,1)S(1)} %copy.51), channel_id=1, source_target_pairs={{0,8},{8,16},{16,24},{24,32},{32,40},{40,48},{48,56},{56,64},{64,7... | collective-permute-start | bytes 786440 | tf_op jit(solution)/shard_map/while/body/eval_jaxpr/ppermute | solution.py:13
  456.2 15.4 %collective-permute-start.1 = (f32[2,512,1,128]{3,1,2,0:T(8,128)S(1)}, f32[2,512,1,128]{3,1,2,0:T(8,128)S(1)}, u32[]{:S(2)}, u32[]{:S(2)}) collective-permute-start(f32[2,512,1,128]{3,1,2,0:T(8,128)S(1)} %convert_add_fusion.3), channel_id=1, source_target_pairs={{0,8},{8,16},{16,24},{24,32},{32,40},{40,48},{48,56},{56,64},{64,7... | collective-permute-start | bytes 1572872 | tf_op jit(solution)/shard_map/while/body/eval_jaxpr/ppermute | solution.py:13
  456.3 15.3 %collective-permute-start = (bf16[2,512,1,128]{3,1,2,0:T(8,128)(2,1)S(1)}, bf16[2,512,1,128]{3,1,2,0:T(8,128)(2,1)S(1)}, u32[]{:S(2)}, u32[]{:S(2)}) collective-permute-start(bf16[2,512,1,128]{3,1,2,0:T(8,128)(2,1)S(1)} %copy.51), channel_id=1, source_target_pairs={{0,8},{8,16},{16,24},{24,32},{32,40},{40,48},{48,56},{56,64},{64,7... | collective-permute-start | bytes 786440 | tf_op jit(solution)/shard_map/while/body/eval_jaxpr/ppermute | solution.py:13
  475.7 15.4 %collective-permute-start.1 = (f32[2,512,1,128]{3,1,2,0:T(8,128)S(1)}, f32[2,512,1,128]{3,1,2,0:T(8,128)S(1)}, u32[]{:S(2)}, u32[]{:S(2)}) collective-permute-start(f32[2,512,1,128]{3,1,2,0:T(8,128)S(1)} %convert_add_fusion.3), channel_id=1, source_target_pairs={{0,8},{8,16},{16,24},{24,32},{32,40},{40,48},{48,56},{56,64},{64,7... | collective-permute-start | bytes 1572872 | tf_op jit(solution)/shard_map/while/body/eval_jaxpr/ppermute | solution.py:13
  475.8 15.3 %collective-permute-start = (bf16[2,512,1,128]{3,1,2,0:T(8,128)(2,1)S(1)}, bf16[2,512,1,128]{3,1,2,0:T(8,128)(2,1)S(1)}, u32[]{:S(2)}, u32[]{:S(2)}) collective-permute-start(bf16[2,512,1,128]{3,1,2,0:T(8,128)(2,1)S(1)} %copy.51), channel_id=1, source_target_pairs={{0,8},{8,16},{16,24},{24,32},{32,40},{40,48},{48,56},{56,64},{64,7... | collective-permute-start | bytes 786440 | tf_op jit(solution)/shard_map/while/body/eval_jaxpr/ppermute | solution.py:13
  495.2 15.4 %collective-permute-start.1 = (f32[2,512,1,128]{3,1,2,0:T(8,128)S(1)}, f32[2,512,1,128]{3,1,2,0:T(8,128)S(1)}, u32[]{:S(2)}, u32[]{:S(2)}) collective-permute-start(f32[2,512,1,128]{3,1,2,0:T(8,128)S(1)} %convert_add_fusion.3), channel_id=1, source_target_pairs={{0,8},{8,16},{16,24},{24,32},{32,40},{40,48},{48,56},{56,64},{64,7... | collective-permute-start | bytes 1572872 | tf_op jit(solution)/shard_map/while/body/eval_jaxpr/ppermute | solution.py:13
  495.3 15.3 %collective-permute-start = (bf16[2,512,1,128]{3,1,2,0:T(8,128)(2,1)S(1)}, bf16[2,512,1,128]{3,1,2,0:T(8,128)(2,1)S(1)}, u32[]{:S(2)}, u32[]{:S(2)}) collective-permute-start(bf16[2,512,1,128]{3,1,2,0:T(8,128)(2,1)S(1)} %copy.51), channel_id=1, source_target_pairs={{0,8},{8,16},{16,24},{24,32},{32,40},{40,48},{48,56},{56,64},{64,7... | collective-permute-start | bytes 786440 | tf_op jit(solution)/shard_map/while/body/eval_jaxpr/ppermute | solution.py:13
  514.7 15.4 %collective-permute-start.1 = (f32[2,512,1,128]{3,1,2,0:T(8,128)S(1)}, f32[2,512,1,128]{3,1,2,0:T(8,128)S(1)}, u32[]{:S(2)}, u32[]{:S(2)}) collective-permute-start(f32[2,512,1,128]{3,1,2,0:T(8,128)S(1)} %convert_add_fusion.3), channel_id=1, source_target_pairs={{0,8},{8,16},{16,24},{24,32},{32,40},{40,48},{48,56},{56,64},{64,7... | collective-permute-start | bytes 1572872 | tf_op jit(solution)/shard_map/while/body/eval_jaxpr/ppermute | solution.py:13
  514.8 15.3 %collective-permute-start = (bf16[2,512,1,128]{3,1,2,0:T(8,128)(2,1)S(1)}, bf16[2,512,1,128]{3,1,2,0:T(8,128)(2,1)S(1)}, u32[]{:S(2)}, u32[]{:S(2)}) collective-permute-start(bf16[2,512,1,128]{3,1,2,0:T(8,128)(2,1)S(1)} %copy.51), channel_id=1, source_target_pairs={{0,8},{8,16},{16,24},{24,32},{32,40},{40,48},{48,56},{56,64},{64,7... | collective-permute-start | bytes 786440 | tf_op jit(solution)/shard_map/while/body/eval_jaxpr/ppermute | solution.py:13
  534.2 15.4 %collective-permute-start.1 = (f32[2,512,1,128]{3,1,2,0:T(8,128)S(1)}, f32[2,512,1,128]{3,1,2,0:T(8,128)S(1)}, u32[]{:S(2)}, u32[]{:S(2)}) collective-permute-start(f32[2,512,1,128]{3,1,2,0:T(8,128)S(1)} %convert_add_fusion.3), channel_id=1, source_target_pairs={{0,8},{8,16},{16,24},{24,32},{32,40},{40,48},{48,56},{56,64},{64,7... | collective-permute-start | bytes 1572872 | tf_op jit(solution)/shard_map/while/body/eval_jaxpr/ppermute | solution.py:13
  534.2 15.3 %collective-permute-start = (bf16[2,512,1,128]{3,1,2,0:T(8,128)(2,1)S(1)}, bf16[2,512,1,128]{3,1,2,0:T(8,128)(2,1)S(1)}, u32[]{:S(2)}, u32[]{:S(2)}) collective-permute-start(bf16[2,512,1,128]{3,1,2,0:T(8,128)(2,1)S(1)} %copy.51), channel_id=1, source_target_pairs={{0,8},{8,16},{16,24},{24,32},{32,40},{40,48},{48,56},{56,64},{64,7... | collective-permute-start | bytes 786440 | tf_op jit(solution)/shard_map/while/body/eval_jaxpr/ppermute | solution.py:13
  553.6 15.4 %collective-permute-start.1 = (f32[2,512,1,128]{3,1,2,0:T(8,128)S(1)}, f32[2,512,1,128]{3,1,2,0:T(8,128)S(1)}, u32[]{:S(2)}, u32[]{:S(2)}) collective-permute-start(f32[2,512,1,128]{3,1,2,0:T(8,128)S(1)} %convert_add_fusion.3), channel_id=1, source_target_pairs={{0,8},{8,16},{16,24},{24,32},{32,40},{40,48},{48,56},{56,64},{64,7... | collective-permute-start | bytes 1572872 | tf_op jit(solution)/shard_map/while/body/eval_jaxpr/ppermute | solution.py:13
  553.7 15.3 %collective-permute-start = (bf16[2,512,1,128]{3,1,2,0:T(8,128)(2,1)S(1)}, bf16[2,512,1,128]{3,1,2,0:T(8,128)(2,1)S(1)}, u32[]{:S(2)}, u32[]{:S(2)}) collective-permute-start(bf16[2,512,1,128]{3,1,2,0:T(8,128)(2,1)S(1)} %copy.51), channel_id=1, source_target_pairs={{0,8},{8,16},{16,24},{24,32},{32,40},{40,48},{48,56},{56,64},{64,7... | collective-permute-start | bytes 786440 | tf_op jit(solution)/shard_map/while/body/eval_jaxpr/ppermute | solution.py:13
  573.1 15.4 %collective-permute-start.1 = (f32[2,512,1,128]{3,1,2,0:T(8,128)S(1)}, f32[2,512,1,128]{3,1,2,0:T(8,128)S(1)}, u32[]{:S(2)}, u32[]{:S(2)}) collective-permute-start(f32[2,512,1,128]{3,1,2,0:T(8,128)S(1)} %convert_add_fusion.3), channel_id=1, source_target_pairs={{0,8},{8,16},{16,24},{24,32},{32,40},{40,48},{48,56},{56,64},{64,7... | collective-permute-start | bytes 1572872 | tf_op jit(solution)/shard_map/while/body/eval_jaxpr/ppermute | solution.py:13
  573.2 15.3 %collective-permute-start = (bf16[2,512,1,128]{3,1,2,0:T(8,128)(2,1)S(1)}, bf16[2,512,1,128]{3,1,2,0:T(8,128)(2,1)S(1)}, u32[]{:S(2)}, u32[]{:S(2)}) collective-permute-start(bf16[2,512,1,128]{3,1,2,0:T(8,128)(2,1)S(1)} %copy.51), channel_id=1, source_target_pairs={{0,8},{8,16},{16,24},{24,32},{32,40},{40,48},{48,56},{56,64},{64,7... | collective-permute-start | bytes 786440 | tf_op jit(solution)/shard_map/while/body/eval_jaxpr/ppermute | solution.py:13
  592.6 15.4 %collective-permute-start.1 = (f32[2,512,1,128]{3,1,2,0:T(8,128)S(1)}, f32[2,512,1,128]{3,1,2,0:T(8,128)S(1)}, u32[]{:S(2)}, u32[]{:S(2)}) collective-permute-start(f32[2,512,1,128]{3,1,2,0:T(8,128)S(1)} %convert_add_fusion.3), channel_id=1, source_target_pairs={{0,8},{8,16},{16,24},{24,32},{32,40},{40,48},{48,56},{56,64},{64,7... | collective-permute-start | bytes 1572872 | tf_op jit(solution)/shard_map/while/body/eval_jaxpr/ppermute | solution.py:13
  592.7 15.3 %collective-permute-start = (bf16[2,512,1,128]{3,1,2,0:T(8,128)(2,1)S(1)}, bf16[2,512,1,128]{3,1,2,0:T(8,128)(2,1)S(1)}, u32[]{:S(2)}, u32[]{:S(2)}) collective-permute-start(bf16[2,512,1,128]{3,1,2,0:T(8,128)(2,1)S(1)} %copy.51), channel_id=1, source_target_pairs={{0,8},{8,16},{16,24},{24,32},{32,40},{40,48},{48,56},{56,64},{64,7... | collective-permute-start | bytes 786440 | tf_op jit(solution)/shard_map/while/body/eval_jaxpr/ppermute | solution.py:13
  612.1 15.4 %collective-permute-start.1 = (f32[2,512,1,128]{3,1,2,0:T(8,128)S(1)}, f32[2,512,1,128]{3,1,2,0:T(8,128)S(1)}, u32[]{:S(2)}, u32[]{:S(2)}) collective-permute-start(f32[2,512,1,128]{3,1,2,0:T(8,128)S(1)} %convert_add_fusion.3), channel_id=1, source_target_pairs={{0,8},{8,16},{16,24},{24,32},{32,40},{40,48},{48,56},{56,64},{64,7... | collective-permute-start | bytes 1572872 | tf_op jit(solution)/shard_map/while/body/eval_jaxpr/ppermute | solution.py:13
  612.2 15.3 %collective-permute-start = (bf16[2,512,1,128]{3,1,2,0:T(8,128)(2,1)S(1)}, bf16[2,512,1,128]{3,1,2,0:T(8,128)(2,1)S(1)}, u32[]{:S(2)}, u32[]{:S(2)}) collective-permute-start(bf16[2,512,1,128]{3,1,2,0:T(8,128)(2,1)S(1)} %copy.51), channel_id=1, source_target_pairs={{0,8},{8,16},{16,24},{24,32},{32,40},{40,48},{48,56},{56,64},{64,7... | collective-permute-start | bytes 786440 | tf_op jit(solution)/shard_map/while/body/eval_jaxpr/ppermute | solution.py:13
  (13 other events, 809.5 us)
Sparse Core Ops, SparseCore 0:
  641.2 111.8 reduce-scatter.1
